TPU v7x, 128 devices: a whole 4x4x4 slice. The times are simulated.
128 devices in a mesh: prow: 8 (over x_hi, z), pcol: 16 (over x_lo, y, core).
Axes of the slice: x: 4 (x_hi: 2, x_lo: 2; x = x_hi * 2 + x_lo), y: 4, z: 4, core: 2. Of those that a mesh axis runs over, the one named last changes fastest.
Arguments:
- left_vecs: bfloat16 [65536, 4096], P(('prow', 'pcol'))
- right_vecs: bfloat16 [65536, 4096], P(('prow', 'pcol'))
- primal: bfloat16 [4096, 4096], P(('prow', 'pcol'))
- dual_inverse: bfloat16 [4096, 4096], P(('prow', 'pcol'))
- owner_map: int32 [128], replicated, may hold values from 0 to 127, each once
- panel_index: int32 [1], replicated, may hold values from 0 to 254
Outputs:
- panel_factor: float32 [256, 65536], P('pcol', 'prow')
- ahead_update: float32 [256, 65536], P('pcol', 'prow')
All inputs are finite; a program needn't handle non-finite values.
Results may differ from a plain program's by a relative error of at most 0.00067.
Values may be sent and summed in bfloat16 or wider, within the bound.
No kernel may reach another device: no remote copies, remote signals or barrier semaphores. Data moves between devices by JAX's collectives and lax.ppermute only.
A program may use at most 128 MiB of HBM per device.

v0:
```python
import jax
import jax.numpy as jnp
from jax import lax
from jax.sharding import PartitionSpec as P

PANEL = 256


def combine(left_prod, right_prod):
    seg = 2 * PANEL
    return (
        left_prod[:, seg : 2 * seg] * right_prod[:, 2 * seg : 3 * seg]
        + right_prod[:, seg : 2 * seg] * left_prod[:, 2 * seg : 3 * seg]
        + left_prod[:, 0:seg] * right_prod[:, 3 * seg : 4 * seg]
        + right_prod[:, 0:seg] * left_prod[:, 3 * seg : 4 * seg]
    )


def relay_rows(first_part, second_part, owner_map, devices, grid_rows):
    slots = first_part.shape[0]
    height = PANEL // devices
    groups = slots // (grid_rows * height)
    grid_cols = devices // grid_rows
    narrow = PANEL // grid_cols
    stacked = jnp.stack([first_part, second_part], axis=1)
    stacked = stacked.reshape(groups, grid_rows, height, 2, grid_cols, narrow)
    outgoing = stacked.transpose(1, 4, 3, 5, 0, 2).reshape(devices, 2, narrow, groups * height)
    arrived = lax.all_to_all(outgoing, ("prow", "pcol"), split_axis=0, concat_axis=0, tiled=True)
    flat = arrived.transpose(1, 2, 0, 3).reshape(2, narrow, devices * groups * height)
    local_rows = slots * devices // grid_rows
    place = jnp.arange(local_rows, dtype=jnp.int32)
    block_num = place // PANEL
    within = place % PANEL
    index = (
        jnp.take(owner_map, within % devices) * (groups * height)
        + block_num * height
        + within // devices
    )
    placed = jnp.take(flat, index, axis=2)
    return (placed[0], placed[1])


def body(left_vecs, right_vecs, primal, dual_inverse, owner_map, panel_index):
    devices = lax.axis_size(("prow", "pcol"))
    grid_rows = lax.axis_size("prow")
    grid_cols = lax.axis_size("pcol")
    per_device = 2 * PANEL // devices
    start = panel_index[0] * PANEL
    first_slot = start // devices
    panel_left = lax.dynamic_slice_in_dim(left_vecs, first_slot, per_device, 0)
    panel_right = lax.dynamic_slice_in_dim(right_vecs, first_slot, per_device, 0)
    panel_pairs = jnp.stack([panel_left, panel_right], axis=1)
    matrices = jnp.stack([primal, dual_inverse], axis=0)
    raw_images = jnp.einsum(
        "gfn,mcn->gfmc",
        matrices,
        lax.all_gather(panel_pairs, ("prow", "pcol"), axis=0, tiled=True),
        preferred_element_type=jnp.float32,
    )
    column_ids = jnp.arange(2 * PANEL, dtype=jnp.int32)
    gathered_ids = jnp.take(owner_map, column_ids % devices) * per_device + column_ids // devices
    ordered = jnp.take(raw_images, gathered_ids, axis=2)
    feature_rows = ordered.shape[1]
    images = ordered.transpose(1, 0, 3, 2).reshape(feature_rows, 8 * PANEL).astype(jnp.bfloat16)
    piece = lax.all_gather(images, ("prow", "pcol"), axis=0, tiled=True)
    left_prod = jnp.dot(left_vecs, piece, preferred_element_type=jnp.float32)
    right_prod = jnp.dot(right_vecs, piece, preferred_element_type=jnp.float32)
    schur = combine(left_prod, right_prod)
    own_panel = lax.dynamic_slice_in_dim(schur, first_slot, per_device, 0)
    panel_block = lax.all_gather(own_panel, ("prow", "pcol"), axis=0, tiled=True)
    panel_block = jnp.take(panel_block, gathered_ids, axis=0)
    chol = jnp.linalg.cholesky(panel_block[:PANEL, :PANEL])
    inverse = lax.linalg.triangular_solve(
        chol, jnp.eye(PANEL, dtype=jnp.float32), left_side=True, lower=True
    )
    ahead = jnp.dot(
        panel_block[PANEL:, :PANEL],
        inverse.T,
        precision=lax.Precision.HIGHEST,
        preferred_element_type=jnp.float32,
    )
    first_cols, second_cols = relay_rows(
        schur[:, :PANEL], schur[:, PANEL:], owner_map, devices, grid_rows
    )
    narrow = PANEL // grid_cols
    my_col = lax.axis_index("pcol")
    through = jnp.dot(
        ahead, inverse, precision=lax.Precision.HIGHEST, preferred_element_type=jnp.float32
    )
    coefficient = jnp.concatenate(
        [
            lax.dynamic_slice_in_dim(inverse, my_col * narrow, narrow, 0),
            lax.dynamic_slice_in_dim(through, my_col * narrow, narrow, 0),
        ],
        axis=0,
    )
    mixed = jnp.dot(
        coefficient,
        lax.all_gather(first_cols, "pcol", axis=0, tiled=True),
        precision=lax.Precision.HIGHEST,
        preferred_element_type=jnp.float32,
    )
    local_rows = first_cols.shape[1]
    place = jnp.arange(local_rows, dtype=jnp.int32)
    schur_ids = (place // PANEL * grid_rows + lax.axis_index("prow")) * PANEL + place % PANEL
    factor_out = jnp.where((schur_ids >= start)[None, :], mixed[:narrow], jnp.float32(0.0))
    update_out = jnp.where(
        (schur_ids >= start + PANEL)[None, :], second_cols - mixed[narrow:], jnp.float32(0.0)
    )
    return (factor_out, update_out)


def solution(mesh):
    return jax.shard_map(
        body,
        mesh=mesh,
        in_specs=(
            P(("prow", "pcol"), None),
            P(("prow", "pcol"), None),
            P(("prow", "pcol"), None),
            P(("prow", "pcol"), None),
            P(),
            P(),
        ),
        out_specs=(P("pcol", "prow"), P("pcol", "prow")),
        check_vma=False,
    )
```

profile of v0, /device:TPU:1, one launch (start us, length us, event | category | flops | bytes accessed | tf_op | source)
XLA Modules:
  0.0 792.8 jit_solution(15497845385659087788)
XLA Ops:
  7.9 1.0 dynamic-slice_bitcast_fusion
  9.0 0.7 copy.28
  9.8 3.3 gather_fusion
  13.2 201.9 %all-gather.7.cloned.1.call-done = bf16[512,2,4096]{2,1,0:T(2,128)(2,1)} async-done(((bf16[4,2,4096]{2,1,0:T(2,128)(2,1)}), bf16[512,2,4096]{2,1,0:T(2,128)(2,1)}) %all-gather.7.cloned.1.call-update) | async-done | bytes 8388624 | tf_op jit(solution)/shard_map/all_gather | solution.py:57
  215.0 12.7 %fusion.2 = bf16[2,32,512,2]{2,1,3,0:T(8,128)(2,1)S(1)} fusion(bf16[512,2,4096]{2,1,0:T(2,128)(2,1)} %all-gather.7.cloned.1.call-done, bf16[1,32,4096]{2,1,0:T(8,128)(2,1)} %bitcast.90, bf16[1,32,4096]{2,1,0:T(8,128)(2,1)} %bitcast.91), kind=kOutput, calls=%fused_computation.10 | convolution fusion | flops 537919488 | bytes 9043968 | tf_op jit(solution)/shard_map/gfn,mcn->gfmc/dot_general | solution.py:54
  228.1 2.3 gather_fusion.1
  230.4 1.8 fusion.11
  232.2 0.7 copy.31
  233.0 0.7 convert_element_type.12
  233.8 49.0 %gather_fusion.3 = s32[8192]{0:T(1024)S(1)} fusion(s32[128]{0:T(128)S(1)} %copy-done, s32[8192]{0:T(1024)S(1)} %broadcast_clamp_fusion.1), kind=kCustom, calls=%fused_computation.3 | custom fusion | bytes 98304 | tf_op jit(solution)/shard_map/jit(_take)/gather | solution.py:35
  282.8 161.4 %all-gather.9.cloned.1.call-done = bf16[4096,2048]{1,0:T(8,128)(2,1)} async-done(((bf16[32,2048]{1,0:T(8,128)(2,1)}), bf16[4096,2048]{1,0:T(8,128)(2,1)}) %all-gather.9.cloned.1.call-update) | async-done | bytes 16777232 | tf_op jit(solution)/shard_map/all_gather | solution.py:65
  444.3 13.0 %convolution_bitcast_fusion = f32[512,2048]{1,0:T(8,128)S(1)} fusion(bf16[512,4096]{1,0:T(8,128)(2,1)} %param.7, bf16[4096,2048]{1,0:T(8,128)(2,1)} %all-gather.9.cloned.1.call-done), kind=kOutput, calls=%fused_computation.13 | convolution fusion | flops 8589934592 | bytes 25165824 | tf_op jit(solution)/shard_map/dot_general | solution.py:67
  457.3 11.5 %convolution_bitcast_fusion.1 = f32[512,2048]{1,0:T(8,128)S(1)} fusion(bf16[512,4096]{1,0:T(8,128)(2,1)S(1)} %copy-done.2, bf16[4096,2048]{1,0:T(8,128)(2,1)} %all-gather.9.cloned.1.call-done), kind=kOutput, calls=%fused_computation.14 | convolution fusion | flops 8589934592 | bytes 25165824 | tf_op jit(solution)/shard_map/dot_general | solution.py:66
  468.8 1.0 fusion.5
  469.9 2.6 stack.33
  472.5 2.6 stack.34
  475.2 8.6 %maximum_bitcast_fusion = f32[8,16,2,16,32,2]{3,1,5,0,4,2:T(8,128)} fusion(f32[32,8,2,1,16,16]{5,4,2,1,0,3:T(8,128)} %stack.34, f32[32,8,2,1,16,16]{5,4,2,1,0,3:T(8,128)} %stack.33), kind=kLoop, calls=%fused_computation.7 | loop fusion | flops 262144 | bytes 2097152 | tf_op jit(solution)/shard_map/transpose | solution.py:27
  483.7 9.4 %copy.34 = f32[8,16,2,16,32,2]{1,0,5,4,3,2:T(8,128)} copy(f32[8,16,2,16,32,2]{3,1,5,0,4,2:T(8,128)} %maximum_bitcast_fusion) | data formatting | bytes 2097152 | tf_op jit(solution)/shard_map/transpose | solution.py:27
  493.1 6.5 reshape.336
  499.6 3.1 copy.35
  502.6 2.3 reshape.402
  504.9 7.1 all-to-all-start
  512.2 0.6 dynamic-slice_bitcast_fusion.2
  513.1 18.4 %all-to-all-done = f32[128,1,2048]{2,1,0:T(1,128)S(1)} async-done(((f32[128,1,2048]{2,1,0:T(1,128)}), f32[128,1,2048]{2,1,0:T(1,128)S(1)}, u32[]{:S(2)}, u32[]{:S(2)}) %all-to-all-start) | async-done | bytes 1048608 | tf_op jit(solution)/shard_map/all_to_all | solution.py:28
  531.5 0.5 broadcast.826
  532.0 3.2 reduce.12
  535.2 0.8 reshape.403
  536.0 7.3 copy.40
  543.4 59.5 %gather_fusion.4 = f32[8192,2,16]{2,1,0:T(2,128)} fusion(f32[2,16,8192]{1,0,2:T(2,128)} %bitcast.82, s32[8192]{0:T(1024)S(1)} %broadcast_clamp_fusion), kind=kCustom, calls=%fused_computation.4 | custom fusion | bytes 2129920 | tf_op jit(solution)/shard_map/jit(_take)/gather | solution.py:39
  602.9 9.3 %copy.38 = f32[8192,2,16]{0,2,1:T(8,128)S(1)} copy(f32[8192,2,16]{2,1,0:T(2,128)} %gather_fusion.4) | data formatting | bytes 2097152 | tf_op jit(solution)/shard_map/jit(_take)/gather | solution.py:39
  612.3 0.8 slice.140
  613.3 98.2 %all-gather.13.cloned.1.call-done = f32[128,4,512]{2,1,0:T(4,128)} async-done(((f32[1,4,512]{2,1,0:T(4,128)}), f32[128,4,512]{2,1,0:T(4,128)}) %all-gather.13.cloned.1.call-update) | async-done | bytes 1048592 | tf_op jit(solution)/shard_map/all_gather | solution.py:70
  711.5 1.6 reshape.399
  713.1 1.6 gather_fusion.2
  715.4 11.7 %cholesky.50 = f32[128,128]{1,0:T(8,128)S(1)} custom-call(f32[128,128]{1,0:T(8,128)S(1)} %cholesky.118), custom_call_target="Cholesky" | custom-call | tf_op jit(solution)/shard_map/jit(cholesky)/cholesky | solution.py:72
  727.2 9.8 %custom-call.14 = f32[1,128,128]{1,2,0:T(8,128)S(1)} custom-call(f32[1,128,128]{2,1,0:T(8,128)S(1)} %get-tuple-element.27), custom_call_target="InvertDiagBlocksLowerTriangular" | custom-call | tf_op jit(solution)/shard_map/jit(cholesky)/cholesky | solution.py:72
  737.5 11.7 %cholesky.105 = f32[128,128]{1,0:T(8,128)S(1)} custom-call(f32[128,128]{1,0:T(8,128)S(1)} %convolution_subtract_fusion.1), custom_call_target="Cholesky" | custom-call | tf_op jit(solution)/shard_map/jit(cholesky)/cholesky | solution.py:72
  749.2 0.6 compare_reduce_fusion
  749.9 0.6 compare_reduce_fusion.1
  751.8 3.8 while.1
  751.8 0.6 fusion.74
  752.4 1.3 bitcast_dynamic-update-slice_fusion.2
  753.8 0.6 fusion.74
  754.4 1.3 bitcast_dynamic-update-slice_fusion.2
  755.7 19.9 %custom-call.15 = f32[2,128,128]{1,2,0:T(8,128)S(1)} custom-call(f32[2,128,128]{2,1,0:T(8,128)S(1)} %get-tuple-element.9), custom_call_target="InvertDiagBlocksLowerTriangular" | custom-call | tf_op jit(solution)/shard_map/triangular_solve | solution.py:73
  776.5 0.6 fusion.12
  777.5 7.2 fusion
  784.7 1.1 fusion.8
  (54 shorter events, 3.9 us)
Async XLA Ops:
  7.2 2.6 copy-start
  7.2 207.9 %all-gather.7.cloned.1.call-start = ((), (), s32[]{:S(2)}) async-start(), calls=%async_computation.1 | async-start | bytes 8454144 | tf_op jit(solution)/shard_map/all_gather | solution.py:57
  9.7 434.5 %all-gather.9.cloned.1.call-start = ((), (), s32[]{:S(2)}) async-start(), calls=%async_computation.2 | async-start | bytes 16908288 | tf_op jit(solution)/shard_map/all_gather | solution.py:65
  444.3 13.0 %copy-start.2 = (bf16[512,4096]{1,0:T(8,128)(2,1)S(1)}, bf16[512,4096]{1,0:T(8,128)(2,1)}, u32[]{:S(2)}) copy-start(bf16[512,4096]{1,0:T(8,128)(2,1)} %param.6) | copy-start | bytes 12582916
  504.9 26.6 %all-to-all-start = ((f32[128,1,2048]{2,1,0:T(1,128)}), f32[128,1,2048]{2,1,0:T(1,128)S(1)}, u32[]{:S(2)}, u32[]{:S(2)}) async-start(f32[128,1,2048]{2,1,0:T(1,128)} %reshape.402), calls=%async_computation | async-start | bytes 2097152 | tf_op jit(solution)/shard_map/all_to_all | solution.py:28
  512.0 199.5 %all-gather.13.cloned.1.call-start = ((), (), s32[]{:S(2)}) async-start(), calls=%async_computation.4 | async-start | bytes 1056768 | tf_op jit(solution)/shard_map/all_gather | solution.py:70
  512.8 264.7 %all-gather.11.cloned.1.call-start = ((), (), s32[]{:S(2)}) async-start(), calls=%async_computation.3 | async-start | bytes 8912896 | tf_op jit(solution)/shard_map/all_gather | solution.py:99
  737.0 48.8 %copy-start.1 = (s32[128]{0:T(128)S(1)}, s32[128]{0:T(128)}, u32[]{:S(2)}) copy-start(s32[128]{0:T(128)} %param.10) | copy-start | bytes 1540
Sparse Core Ops, SparseCore 0:
  10.3 204.7 all-gather.6
  233.9 210.3 all-gather.8
  515.1 196.3 all-gather.12
  713.6 51.2 all-gather.10
where the time goes:
time: 802 us; the launch traced here: 793 us
  waiting for transfers between devices  480 us (60%)
  local copies, waits for them, and re-layouts  171 us (21%)
  other arithmetic  70.8 us (9%)
  matrix products  46.7 us (6%)
  between operations  16.6 us (2%)
    all_gather x1, waiting for transfers between devices, body(): lax.all_gather(panel_pairs, ('prow', 'pcol'), axis=0, tiled=True)  202 us
    all_gather x1, waiting for transfers between devices, body(): piece = lax.all_gather(images, ('prow', 'pcol'), axis=0, tiled=True)  161 us
    all_gather x1, waiting for transfers between devices, body(): lax.all_gather(own_panel, ('prow', 'pcol'), axis=0, tiled=True)  98.2 us
    gather x2, local copies, waits for them, and re-layouts, relay_rows(): placed = jnp.take(flat, index, axis=2)  68.8 us
    gather x1, local copies, waits for them, and re-layouts, relay_rows(): jnp.take(owner_map, within % devices) * (groups * height)  49 us
    another operation x7, other arithmetic, body(): chol = jnp.linalg.cholesky(panel_block[:PANEL, :PANEL])  34.6 us
    another operation x4, other arithmetic, body(): lax.linalg.triangular_solve(chol, jnp.eye(PANEL, dtype=jnp.float32), left...  20 us
    all_to_all x1, waiting for transfers between devices, relay_rows(): lax.all_to_all(outgoing, ('prow', 'pcol'), split_axis=0, concat_axis=0, t...  18.4 us
  transfers between devices with their start and end apart: 5, of which 4 were waited for; matrix products, arithmetic and copies ran while one was open for 25% of the time, Pallas kernels for 0%

commit v1 on v0

v1 whole, which is shorter than its diff:
```python
import jax
import jax.numpy as jnp
from jax import lax
from jax.sharding import PartitionSpec as P

PANEL = 256


def combine(left_prod, right_prod):
    seg = 2 * PANEL
    return (
        left_prod[:, seg : 2 * seg] * right_prod[:, 2 * seg : 3 * seg]
        + right_prod[:, seg : 2 * seg] * left_prod[:, 2 * seg : 3 * seg]
        + left_prod[:, 0:seg] * right_prod[:, 3 * seg : 4 * seg]
        + right_prod[:, 0:seg] * left_prod[:, 3 * seg : 4 * seg]
    )


def gather_all(x):
    x = lax.all_gather(x, "pcol", axis=0, tiled=True)
    return lax.all_gather(x, "prow", axis=0, tiled=True)


def relay_rows(first_part, second_part, owner_map, devices, grid_rows):
    slots = first_part.shape[0]
    height = PANEL // devices
    groups = slots // (grid_rows * height)
    grid_cols = devices // grid_rows
    narrow = PANEL // grid_cols
    stacked = jnp.stack([first_part, second_part], axis=1)
    stacked = stacked.reshape(groups, grid_rows, height, 2, grid_cols, narrow)
    outgoing = stacked.transpose(1, 4, 3, 5, 0, 2).reshape(devices, 2 * narrow * groups * height)
    arrived = lax.all_to_all(outgoing, ("prow", "pcol"), split_axis=0, concat_axis=0, tiled=True)
    ordered = jnp.take(arrived, owner_map, axis=0)
    ordered = ordered.reshape(devices, 2, narrow, groups, height)
    placed = ordered.transpose(1, 2, 3, 4, 0).reshape(2, narrow, groups * height * devices)
    return (placed[0], placed[1])


def body(left_vecs, right_vecs, primal, dual_inverse, owner_map, panel_index):
    devices = lax.axis_size(("prow", "pcol"))
    grid_rows = lax.axis_size("prow")
    grid_cols = lax.axis_size("pcol")
    per_device = 2 * PANEL // devices
    start = panel_index[0] * PANEL
    first_slot = start // devices
    me = lax.axis_index("prow") * grid_cols + lax.axis_index("pcol")
    residue = jnp.sum(jnp.where(owner_map == me, jnp.arange(devices, dtype=jnp.int32), 0))
    panel_left = lax.dynamic_slice_in_dim(left_vecs, first_slot, per_device, 0)
    panel_right = lax.dynamic_slice_in_dim(right_vecs, first_slot, per_device, 0)
    panel_pairs = jnp.stack([panel_left, panel_right], axis=1)
    matrices = jnp.stack([primal, dual_inverse], axis=0)
    raw_images = jnp.einsum(
        "gfn,mcn->gfmc",
        matrices,
        gather_all(panel_pairs),
        preferred_element_type=jnp.float32,
    )
    column_ids = jnp.arange(2 * PANEL, dtype=jnp.int32)
    gathered_ids = jnp.take(owner_map, column_ids % devices) * per_device + column_ids // devices
    ordered = jnp.take(raw_images, gathered_ids, axis=2)
    feature_rows = ordered.shape[1]
    images = ordered.transpose(1, 0, 3, 2).reshape(feature_rows, 8 * PANEL).astype(jnp.bfloat16)
    piece = gather_all(images)
    left_prod = jnp.dot(left_vecs, piece, preferred_element_type=jnp.float32)
    right_prod = jnp.dot(right_vecs, piece, preferred_element_type=jnp.float32)
    schur = combine(left_prod, right_prod)
    own_panel = lax.dynamic_slice_in_dim(schur[:, :PANEL], first_slot, per_device, 0)
    panel_block = gather_all(own_panel)
    panel_block = jnp.take(panel_block, gathered_ids, axis=0)
    chol = jnp.linalg.cholesky(panel_block[:PANEL])
    inverse = lax.linalg.triangular_solve(
        chol, jnp.eye(PANEL, dtype=jnp.float32), left_side=True, lower=True
    )
    ahead = jnp.dot(
        panel_block[PANEL:],
        inverse.T,
        precision=lax.Precision.HIGHEST,
        preferred_element_type=jnp.float32,
    )
    slots = schur.shape[0]
    schur_ids = jnp.arange(slots, dtype=jnp.int32) * devices + residue
    full = jnp.dot(
        schur[:, :PANEL],
        inverse.T,
        precision=lax.Precision.HIGHEST,
        preferred_element_type=jnp.float32,
    )
    full = jnp.where((schur_ids >= start)[:, None], full, jnp.float32(0.0))
    update = schur[:, PANEL:] - jnp.dot(
        full, ahead.T, precision=lax.Precision.HIGHEST, preferred_element_type=jnp.float32
    )
    update = jnp.where((schur_ids >= start + PANEL)[:, None], update, jnp.float32(0.0))
    return relay_rows(full, update, owner_map, devices, grid_rows)


def solution(mesh):
    return jax.shard_map(
        body,
        mesh=mesh,
        in_specs=(
            P(("prow", "pcol"), None),
            P(("prow", "pcol"), None),
            P(("prow", "pcol"), None),
            P(("prow", "pcol"), None),
            P(),
            P(),
        ),
        out_specs=(P("pcol", "prow"), P("pcol", "prow")),
        check_vma=False,
    )
```

time: 802 us -> 595 us (0.74); the launches traced: 793 us -> 594 us
  local copies, waits for them, and re-layouts: 171 us -> 44.4 us
  waiting for transfers between devices: 480 us -> 373 us
  blocking collectives: 0 us -> 49.6 us
  matrix products: 46.7 us -> 33.7 us
    gather x3 -> x2, local copies, waits for them, and re-layouts: 118 us -> 1.3 us  [relay_rows(): ordered = jnp.take(arrived, owner_map, axis=0)]
    all_gather x4, waiting for transfers between devices: 462 us -> 353 us  [the longest x2 284 us: gather_all(): return lax.all_gather(x, 'prow', axis=0, tiled=True)]
    all_gather x0 -> x2, blocking collectives: none -> 49.6 us  [the longest x1 29.6 us: gather_all(): return lax.all_gather(x, 'prow', axis=0, tiled=True)]
    reshape x3 -> x0, local copies, waits for them, and re-layouts: 16.8 us -> none  [the longest x2 9.51 us: relay_rows(): stacked.transpose(1, 4, 3, 5, 0, 2)]
    dot_general x4, matrix products: 20.9 us -> 7.87 us  [the longest x1 6.04 us: body(): jnp.einsum('gfn,mcn->gfmc', matrices, gather_all(panel_pairs), preferred_...]
    another operation x4 -> x3, other arithmetic: 20 us -> 19.9 us  [body(): lax.linalg.triangular_solve(chol, jnp.eye(PANEL, dtype=jnp.float32), left...]
  transfers between devices with their start and end apart: 5 -> 5, of which waited for: 4 -> 5; matrix products, arithmetic and copies ran while one was open for 25% -> 1% of each run, Pallas kernels for 0% -> 0%
where the time goes in v1:
time: 595 us; the launch traced here: 594 us
  waiting for transfers between devices  373 us (63%)
  other arithmetic  67.9 us (11%)
  blocking collectives  49.6 us (8%)
  local copies, waits for them, and re-layouts  44.4 us (7%)
  matrix products  33.7 us (6%)
  between operations  16.2 us (3%)
  starting transfers between devices  9.34 us (2%)
    all_gather x2, waiting for transfers between devices, gather_all(): return lax.all_gather(x, 'prow', axis=0, tiled=True)  284 us
    all_gather x2, waiting for transfers between devices, gather_all(): x = lax.all_gather(x, 'pcol', axis=0, tiled=True)  69.1 us
    another operation x7, other arithmetic, body(): chol = jnp.linalg.cholesky(panel_block[:PANEL])  34.6 us
    all_gather x1, blocking collectives, gather_all(): return lax.all_gather(x, 'prow', axis=0, tiled=True)  29.6 us
    all_gather x1, blocking collectives, gather_all(): x = lax.all_gather(x, 'pcol', axis=0, tiled=True)  20.1 us
    another operation x3, other arithmetic, body(): lax.linalg.triangular_solve(chol, jnp.eye(PANEL, dtype=jnp.float32), left...  19.9 us
    all_to_all x1, waiting for transfers between devices, relay_rows(): lax.all_to_all(outgoing, ('prow', 'pcol'), split_axis=0, concat_axis=0, t...  19.6 us
    dot_general x1, matrix products, body(): right_prod = jnp.dot(right_vecs, piece, preferred_element_type=jnp.float32)  13 us
  transfers between devices with their start and end apart: 5, of which 5 were waited for; matrix products, arithmetic and copies ran while one was open for 1% of the time, Pallas kernels for 0%

profile of v1, /device:TPU:1, one launch (start us, length us, event | category | flops | bytes accessed | tf_op | source)
XLA Modules:
  0.0 594.3 jit_solution(6907787389066735002)
XLA Ops:
  8.0 1.0 dynamic-slice_bitcast_fusion
  9.0 0.7 copy.28
  9.8 36.3 %all-gather.6.cloned.1.call-done = bf16[64,2,4096]{2,1,0:T(2,128)(2,1)} async-done(((bf16[4,2,4096]{2,1,0:T(2,128)(2,1)}), bf16[64,2,4096]{2,1,0:T(2,128)(2,1)}) %all-gather.6.cloned.1.call-update) | async-done | bytes 1048592 | tf_op jit(solution)/shard_map/all_gather | solution.py:20
  46.1 2.9 copy.29
  49.1 3.3 gather_fusion
  52.5 102.2 %all-gather.8.cloned.1.call-done = bf16[512,2,4096]{2,0,1:T(8,128)(2,1)} async-done(((bf16[64,2,4096]{2,0,1:T(8,128)(2,1)}), bf16[512,2,4096]{2,0,1:T(8,128)(2,1)}) %all-gather.8.cloned.1.call-update) | async-done | bytes 8388624 | tf_op jit(solution)/shard_map/all_gather | solution.py:21
  154.7 6.0 %fusion = bf16[2,32,512,2]{2,1,3,0:T(8,128)(2,1)S(1)} fusion(bf16[512,2,4096]{2,0,1:T(8,128)(2,1)} %all-gather.8.cloned.1.call-done, bf16[1,32,4096]{2,1,0:T(8,128)(2,1)S(1)} %bitcast.77, bf16[1,32,4096]{2,1,0:T(8,128)(2,1)S(1)} %bitcast.78), kind=kOutput, calls=%fused_computation.7 | convolution fusion | flops 537919488 | bytes 9043968 | tf_op jit(solution)/shard_map/gfn,mcn->gfmc/dot_general | solution.py:53
  160.8 0.4 copy.30
  161.2 2.3 gather_fusion.1
  163.5 1.8 fusion.8
  165.2 0.7 copy.31
  166.0 0.7 convert_element_type.12
  166.8 32.8 %all-gather.10.cloned.1.call-done = bf16[512,2048]{1,0:T(8,128)(2,1)} async-done(((bf16[32,2048]{1,0:T(8,128)(2,1)}), bf16[512,2048]{1,0:T(8,128)(2,1)}) %all-gather.10.cloned.1.call-update) | async-done | bytes 2097168 | tf_op jit(solution)/shard_map/all_gather | solution.py:20
  199.6 0.6 compare_select_fusion.4
  200.3 0.7 fusion.24
  200.9 182.1 %all-gather.12.cloned.1.call-done = bf16[4096,2048]{1,0:T(8,128)(2,1)} async-done(((bf16[512,2048]{1,0:T(8,128)(2,1)}), bf16[4096,2048]{1,0:T(8,128)(2,1)}) %all-gather.12.cloned.1.call-update) | async-done | bytes 16777232 | tf_op jit(solution)/shard_map/all_gather | solution.py:21
  383.1 13.0 %convolution_bitcast_fusion = f32[512,2048]{1,0:T(8,128)S(1)} fusion(bf16[512,4096]{1,0:T(8,128)(2,1)} %param.7, bf16[4096,2048]{1,0:T(8,128)(2,1)} %all-gather.12.cloned.1.call-done), kind=kOutput, calls=%fused_computation.9 | convolution fusion | flops 8589934592 | bytes 25165824 | tf_op jit(solution)/shard_map/dot_general | solution.py:66
  396.0 11.5 %convolution_bitcast_fusion.1 = f32[512,2048]{1,0:T(8,128)S(1)} fusion(bf16[512,4096]{1,0:T(8,128)(2,1)S(1)} %copy-done.3, bf16[4096,2048]{1,0:T(8,128)(2,1)} %all-gather.12.cloned.1.call-done), kind=kOutput, calls=%fused_computation.10 | convolution fusion | flops 8589934592 | bytes 25165824 | tf_op jit(solution)/shard_map/dot_general | solution.py:65
  407.6 1.0 fusion.3
  408.7 20.1 %all-gather = f32[16,4,256]{2,1,0:T(4,128)S(1)} all-gather(f32[1,4,256]{2,1,0:T(4,128)S(1)} %dynamic-slice_bitcast_fusion.2), channel_id=1, replica_groups=mesh['prow'=8,'pcol'=16] {'pcol'}, dimensions={0}, use_global_device_ids=true | all-gather | bytes 69632 | tf_op jit(solution)/shard_map/all_gather | solution.py:20
  428.8 29.6 %all_gather.23 = f32[512,256]{1,0:T(8,128)S(1)} all-gather(f32[64,256]{1,0:T(8,128)S(1)} %reshape.214), channel_id=1, replica_groups=mesh['prow'=8,'pcol'=16] {'prow'}, dimensions={0}, use_global_device_ids=true | all-gather | bytes 589824 | tf_op jit(solution)/shard_map/all_gather | solution.py:21
  458.4 1.6 gather_fusion.2
  460.4 11.7 %cholesky.50 = f32[128,128]{1,0:T(8,128)S(1)} custom-call(f32[128,128]{1,0:T(8,128)S(1)} %cholesky.118), custom_call_target="Cholesky" | custom-call | tf_op jit(solution)/shard_map/jit(cholesky)/cholesky | solution.py:71
  472.2 9.8 %custom-call.14 = f32[1,128,128]{1,2,0:T(8,128)S(1)} custom-call(f32[1,128,128]{2,1,0:T(8,128)S(1)} %get-tuple-element.25), custom_call_target="InvertDiagBlocksLowerTriangular" | custom-call | tf_op jit(solution)/shard_map/jit(cholesky)/cholesky | solution.py:71
  482.5 11.7 %cholesky.105 = f32[128,128]{1,0:T(8,128)S(1)} custom-call(f32[128,128]{1,0:T(8,128)S(1)} %convolution_subtract_fusion.2), custom_call_target="Cholesky" | custom-call | tf_op jit(solution)/shard_map/jit(cholesky)/cholesky | solution.py:71
  494.2 0.6 compare_reduce_fusion
  494.9 0.6 compare_reduce_fusion.1
  496.9 4.0 while.1
  496.9 0.6 fusion.46
  497.5 1.4 bitcast_dynamic-update-slice_fusion.2
  498.9 0.6 fusion.46
  499.5 1.4 bitcast_dynamic-update-slice_fusion.2
  500.9 19.9 %custom-call.15 = f32[2,128,128]{1,2,0:T(8,128)S(1)} custom-call(f32[2,128,128]{2,1,0:T(8,128)S(1)} %get-tuple-element.9), custom_call_target="InvertDiagBlocksLowerTriangular" | custom-call | tf_op jit(solution)/shard_map/triangular_solve | solution.py:72
  521.7 0.6 fusion.9
  522.3 0.6 convolution_select_fusion
  522.9 2.6 stack.33
  525.5 0.6 fusion.2
  526.1 2.6 stack.34
  528.8 8.6 %maximum_bitcast_fusion = f32[8,16,2,16,32,2]{3,1,5,0,4,2:T(8,128)} fusion(f32[32,8,2,1,16,16]{5,4,2,1,0,3:T(8,128)} %stack.34, f32[32,8,2,1,16,16]{5,4,2,1,0,3:T(8,128)} %stack.33), kind=kLoop, calls=%fused_computation.6 | loop fusion | flops 262144 | bytes 2097152 | tf_op jit(solution)/shard_map/transpose | solution.py:32
  537.3 9.3 %copy.34 = f32[8,16,2,16,32,2]{1,0,5,4,3,2:T(8,128)} copy(f32[8,16,2,16,32,2]{3,1,5,0,4,2:T(8,128)} %maximum_bitcast_fusion) | data formatting | bytes 2097152 | tf_op jit(solution)/shard_map/transpose | solution.py:32
  546.7 5.6 all_to_all.8
  552.3 1.9 copy.35
  554.2 9.2 %all-to-all-start = ((f32[128,1,2048]{2,1,0:T(1,128)}), f32[128,1,2048]{2,1,0:T(1,128)S(1)}, u32[]{:S(2)}, u32[]{:S(2)}) async-start(f32[128,1,2048]{2,1,0:T(1,128)} %copy.35), calls=%async_computation | async-start | bytes 2097152 | tf_op jit(solution)/shard_map/all_to_all | solution.py:33
  563.4 19.6 %all-to-all-done = f32[128,1,2048]{2,1,0:T(1,128)S(1)} async-done(((f32[128,1,2048]{2,1,0:T(1,128)}), f32[128,1,2048]{2,1,0:T(1,128)S(1)}, u32[]{:S(2)}, u32[]{:S(2)}) %all-to-all-start) | async-done | bytes 1048608 | tf_op jit(solution)/shard_map/all_to_all | solution.py:33
  583.4 1.0 gather_fusion.3
  584.7 0.5 select_bitcast_fusion
  585.4 1.2 squeeze.7
  586.6 1.2 squeeze.8
  (51 shorter events, 3.2 us)
Async XLA Ops:
  7.2 41.9 %copy-start = (s32[128]{0:T(128)S(1)}, s32[128]{0:T(128)}, u32[]{:S(2)}) copy-start(s32[128]{0:T(128)} %param.10) | copy-start | bytes 1540
  7.2 147.5 %copy-start.2 = (bf16[32,4096]{1,0:T(8,128)(2,1)S(1)}, bf16[32,4096]{1,0:T(8,128)(2,1)}, u32[]{:S(2)}) copy-start(bf16[32,4096]{1,0:T(8,128)(2,1)} %param.8) | copy-start | bytes 786436
  7.2 147.5 %copy-start.1 = (bf16[32,4096]{1,0:T(8,128)(2,1)S(1)}, bf16[32,4096]{1,0:T(8,128)(2,1)}, u32[]{:S(2)}) copy-start(bf16[32,4096]{1,0:T(8,128)(2,1)} %param.9) | copy-start | bytes 786436
  7.2 38.9 %all-gather.6.cloned.1.call-start = ((), (), s32[]{:S(2)}) async-start(), calls=%async_computation.1 | async-start | bytes 1114112 | tf_op jit(solution)/shard_map/all_gather | solution.py:20
  9.8 144.9 %all-gather.8.cloned.1.call-start = ((), (), s32[]{:S(2)}) async-start(), calls=%async_computation.2 | async-start | bytes 9437184 | tf_op jit(solution)/shard_map/all_gather | solution.py:21
  49.0 150.6 %all-gather.10.cloned.1.call-start = ((), (), s32[]{:S(2)}) async-start(), calls=%async_computation.3 | async-start | bytes 2228224 | tf_op jit(solution)/shard_map/all_gather | solution.py:20
  166.8 216.3 %all-gather.12.cloned.1.call-start = ((), (), s32[]{:S(2)}) async-start(), calls=%async_computation.4 | async-start | bytes 18874368 | tf_op jit(solution)/shard_map/all_gather | solution.py:21
  383.0 13.0 %copy-start.3 = (bf16[512,4096]{1,0:T(8,128)(2,1)S(1)}, bf16[512,4096]{1,0:T(8,128)(2,1)}, u32[]{:S(2)}) copy-start(bf16[512,4096]{1,0:T(8,128)(2,1)} %param.6) | copy-start | bytes 12582916
  554.2 28.8 %all-to-all-start = ((f32[128,1,2048]{2,1,0:T(1,128)}), f32[128,1,2048]{2,1,0:T(1,128)S(1)}, u32[]{:S(2)}, u32[]{:S(2)}) async-start(f32[128,1,2048]{2,1,0:T(1,128)} %copy.35), calls=%async_computation | async-start | bytes 2097152 | tf_op jit(solution)/shard_map/all_to_all | solution.py:33
Sparse Core Ops, SparseCore 0:
  10.3 35.7 all-gather.5
  49.1 105.5 all-gather.7
  166.9 32.6 all-gather.9
  201.8 181.2 all-gather.11

commit v2 on v1

--- a/solution.py
+++ b/solution.py
@@ -7,7 +7,7 @@
 
 
 def combine(left_prod, right_prod):
-    seg = 2 * PANEL
+    seg = left_prod.shape[1] // 4
     return (
         left_prod[:, seg : 2 * seg] * right_prod[:, 2 * seg : 3 * seg]
         + right_prod[:, seg : 2 * seg] * left_prod[:, 2 * seg : 3 * seg]
@@ -17,8 +17,8 @@
 
 
 def gather_all(x):
-    x = lax.all_gather(x, "pcol", axis=0, tiled=True)
-    return lax.all_gather(x, "prow", axis=0, tiled=True)
+    x = lax.all_gather(x, "prow", axis=0, tiled=True)
+    return lax.all_gather(x, "pcol", axis=0, tiled=True)
 
 
 def relay_rows(first_part, second_part, owner_map, devices, grid_rows):
@@ -50,24 +50,34 @@
     panel_right = lax.dynamic_slice_in_dim(right_vecs, first_slot, per_device, 0)
     panel_pairs = jnp.stack([panel_left, panel_right], axis=1)
     matrices = jnp.stack([primal, dual_inverse], axis=0)
+    gathered_pairs = gather_all(panel_pairs)
     raw_images = jnp.einsum(
-        "gfn,mcn->gfmc",
-        matrices,
-        gather_all(panel_pairs),
-        preferred_element_type=jnp.float32,
+        "gfn,mcn->gfmc", matrices, gathered_pairs, preferred_element_type=jnp.float32
     )
     column_ids = jnp.arange(2 * PANEL, dtype=jnp.int32)
-    gathered_ids = jnp.take(owner_map, column_ids % devices) * per_device + column_ids // devices
+    owners = jnp.take(owner_map, column_ids % devices)
+    gathered_ids = (
+        (owners % grid_cols) * grid_rows + owners // grid_cols
+    ) * per_device + column_ids // devices
     ordered = jnp.take(raw_images, gathered_ids, axis=2)
     feature_rows = ordered.shape[1]
     images = ordered.transpose(1, 0, 3, 2).reshape(feature_rows, 8 * PANEL).astype(jnp.bfloat16)
     piece = gather_all(images)
-    left_prod = jnp.dot(left_vecs, piece, preferred_element_type=jnp.float32)
-    right_prod = jnp.dot(right_vecs, piece, preferred_element_type=jnp.float32)
+
+    def feature_order(vecs):
+        rows = vecs.shape[0]
+        vecs = vecs.reshape(rows, grid_rows, grid_cols, feature_rows)
+        return vecs.transpose(0, 2, 1, 3).reshape(rows, grid_rows * grid_cols * feature_rows)
+
+    left_prod = jnp.dot(feature_order(left_vecs), piece, preferred_element_type=jnp.float32)
+    right_prod = jnp.dot(feature_order(right_vecs), piece, preferred_element_type=jnp.float32)
     schur = combine(left_prod, right_prod)
-    own_panel = lax.dynamic_slice_in_dim(schur[:, :PANEL], first_slot, per_device, 0)
-    panel_block = gather_all(own_panel)
-    panel_block = jnp.take(panel_block, gathered_ids, axis=0)
+    panel_vecs = jnp.take(gathered_pairs, gathered_ids, axis=0)
+    half = piece.reshape(piece.shape[0], 4, 2 * PANEL)[:, :, :PANEL].reshape(piece.shape[0], 4 * PANEL)
+    panel_block = combine(
+        jnp.dot(feature_order(panel_vecs[:, 0]), half, preferred_element_type=jnp.float32),
+        jnp.dot(feature_order(panel_vecs[:, 1]), half, preferred_element_type=jnp.float32),
+    )
     chol = jnp.linalg.cholesky(panel_block[:PANEL])
     inverse = lax.linalg.triangular_solve(
         chol, jnp.eye(PANEL, dtype=jnp.float32), left_side=True, lower=True

time: 595 us -> 530 us (0.89); the launches traced: 594 us -> 523 us
  waiting for transfers between devices: 373 us -> 120 us
  local copies, waits for them, and re-layouts: 44.4 us -> 219 us
  blocking collectives: 49.6 us -> 31.5 us
  matrix products: 33.7 us -> 47.5 us
  other arithmetic: 67.9 us -> 78.9 us
    all_gather x4 -> x3, waiting for transfers between devices: 353 us -> 101 us  [the longest x2 55.9 us: gather_all(): return lax.all_gather(x, 'pcol', axis=0, tiled=True)]
    slice x1 -> x4, local copies, waits for them, and re-layouts: 0.04 us -> 64.6 us  [the longest x2 38.2 us: body(): panel_vecs[:, 1]]
    gather x3 -> x2, local copies, waits for them, and re-layouts: 5.11 us -> 33.3 us  [the longest x1 29.9 us: body(): panel_vecs = jnp.take(gathered_pairs, gathered_ids, axis=0)]
    reshape x0 -> x1, local copies, waits for them, and re-layouts: none -> 27.8 us  [body(): piece.reshape(piece.shape[0], 4, 2 * PANEL)[:, :, :PANEL]]
    unnamed x11 -> x14, local copies, waits for them, and re-layouts: 0.39 us -> 22.8 us
    all_gather x2 -> x1, blocking collectives: 49.6 us -> 31.5 us  [gather_all(): x = lax.all_gather(x, 'prow', axis=0, tiled=True)]
    transpose x0 -> x4, local copies, waits for them, and re-layouts: none -> 16.9 us  [feature_order(): vecs.transpose(0, 2, 1, 3)]
    all_gather x1 -> x2, local copies, waits for them, and re-layouts: 2.86 us -> 17.6 us  [the longest x1 16.5 us: gather_all(): return lax.all_gather(x, 'pcol', axis=0, tiled=True)]
  transfers between devices with their start and end apart: 5 -> 4, of which waited for: 5 -> 3; matrix products, arithmetic and copies ran while one was open for 1% -> 28% of each run, Pallas kernels for 0% -> 0%
where the time goes in v2:
time: 530 us; the launch traced here: 523 us
  local copies, waits for them, and re-layouts  219 us (41%)
  waiting for transfers between devices  120 us (23%)
  other arithmetic  78.9 us (15%)
  matrix products  47.5 us (9%)
  blocking collectives  31.5 us (6%)
  between operations  16.6 us (3%)
  starting transfers between devices  9.03 us (2%)
    all_gather x2, waiting for transfers between devices, gather_all(): return lax.all_gather(x, 'pcol', axis=0, tiled=True)  55.9 us
    all_gather x1, waiting for transfers between devices, gather_all(): x = lax.all_gather(x, 'prow', axis=0, tiled=True)  45 us
    slice x2, local copies, waits for them, and re-layouts, body(): panel_vecs[:, 1]  38.2 us
    another operation x7, other arithmetic, body(): chol = jnp.linalg.cholesky(panel_block[:PANEL])  34.8 us
    all_gather x1, blocking collectives, gather_all(): x = lax.all_gather(x, 'prow', axis=0, tiled=True)  31.5 us
    gather x1, local copies, waits for them, and re-layouts, body(): panel_vecs = jnp.take(gathered_pairs, gathered_ids, axis=0)  29.9 us
    reshape x1, local copies, waits for them, and re-layouts, body(): piece.reshape(piece.shape[0], 4, 2 * PANEL)[:, :, :PANEL]  27.8 us
    unnamed x14, local copies, waits for them, and re-layouts  22.8 us
  transfers between devices with their start and end apart: 4, of which 3 were waited for; matrix products, arithmetic and copies ran while one was open for 28% of the time, Pallas kernels for 0%

profile of v2, /device:TPU:1, one launch (start us, length us, event | category | flops | bytes accessed | tf_op | source)
XLA Modules:
  0.0 522.7 jit_solution(16392603243289183377)
XLA Ops:
  7.9 1.0 dynamic-slice_bitcast_fusion
  9.0 31.5 %all_gather.12 = bf16[32,2,4096]{2,1,0:T(2,128)(2,1)S(1)} all-gather(bf16[4,2,4096]{2,1,0:T(2,128)(2,1)S(1)} %copy.77), channel_id=1, replica_groups=mesh['prow'=8,'pcol'=16] {'prow'}, dimensions={0}, use_global_device_ids=true | all-gather | bytes 589824 | tf_op jit(solution)/shard_map/all_gather | solution.py:20
  40.5 1.1 copy.78
  41.7 3.4 gather_fusion
  45.2 55.9 %all-gather.4.cloned.1.call-done = bf16[512,2,4096]{2,0,1:T(8,128)(2,1)} async-done(((bf16[32,2,4096]{2,0,1:T(8,128)(2,1)}), bf16[512,2,4096]{2,0,1:T(8,128)(2,1)}) %all-gather.4.cloned.1.call-update) | async-done | bytes 8388624 | tf_op jit(solution)/shard_map/all_gather | solution.py:21
  101.1 6.2 %fusion = bf16[2,32,512,2]{2,1,3,0:T(8,128)(2,1)S(1)} fusion(bf16[512,2,4096]{2,0,1:T(8,128)(2,1)} %all-gather.4.cloned.1.call-done, bf16[1,32,4096]{2,1,0:T(8,128)(2,1)} %bitcast.108, bf16[1,32,4096]{2,1,0:T(8,128)(2,1)} %bitcast.109), kind=kOutput, calls=%fused_computation.8 | convolution fusion | flops 537919488 | bytes 9043968 | tf_op jit(solution)/shard_map/gfn,mcn->gfmc/dot_general | solution.py:54
  107.7 2.3 gather_fusion.1
  110.0 1.8 fusion.12
  111.8 0.7 copy.80
  113.8 45.0 %all-gather.6.cloned.1.call-done = bf16[256,2048]{1,0:T(8,128)(2,1)} async-done(((bf16[32,2048]{1,0:T(8,128)(2,1)}), bf16[256,2048]{1,0:T(8,128)(2,1)}) %all-gather.6.cloned.1.call-update) | async-done | bytes 1048592 | tf_op jit(solution)/shard_map/all_gather | solution.py:20
  158.9 6.5 %copy.81 = bf16[512,4096]{0,1:T(8,128)(2,1)} copy(bf16[512,4096]{1,0:T(8,128)(2,1)} %param.6) | data formatting | bytes 8388608 | tf_op args[0]
  165.4 6.6 %copy.83 = bf16[512,4096]{0,1:T(8,128)(2,1)} copy(bf16[512,4096]{1,0:T(8,128)(2,1)} %param.7) | data formatting | bytes 8388608 | tf_op args[1]
  172.0 4.9 copy.82
  176.9 2.4 copy.84
  180.7 16.5 %copy.85 = bf16[512,2,4096]{2,1,0:T(2,128)(2,1)} copy(bf16[512,2,4096]{2,0,1:T(8,128)(2,1)} %all-gather.4.cloned.1.call-done) | data formatting | bytes 16777216 | tf_op jit(solution)/shard_map/all_gather | solution.py:21
  197.2 29.9 %gather_fusion.2 = bf16[512,2,4096]{2,1,0:T(2,128)(2,1)} fusion(bf16[512,2,4096]{2,1,0:T(2,128)(2,1)} %copy.85, s32[1024]{0:T(1024)S(1)} %pad_clamp_fusion.1), kind=kCustom, calls=%fused_computation.2 | custom fusion | bytes 16779264 | tf_op jit(solution)/shard_map/jit(_take)/gather | solution.py:75
  227.0 10.5 %broadcast_select_fusion = bf16[512,2,4096]{2,1,0:T(2,128)(2,1)S(1)} fusion(bf16[512,2,4096]{2,1,0:T(2,128)(2,1)} %gather_fusion.2, pred[512]{0:T(512)(128)(4,1)S(1)} %compare_and_fusion), kind=kLoop, calls=%fused_computation.6 | loop fusion | flops 4194304 | bytes 16777728 | tf_op jit(solution)/shard_map/jit(_take)/select_n | solution.py:75
  237.6 19.9 %fusion.44 = (bf16[512,1,4096]{2,1,0:T(2,128)(2,1)}, bf16[512,1,4096]{2,1,0:T(2,128)(2,1)}) fusion(bf16[512,2,4096]{2,1,0:T(2,128)(2,1)S(1)} %broadcast_select_fusion), kind=kLoop, calls=%fused_computation.124 | loop fusion | bytes 16777216 | tf_op jit(solution)/shard_map/slice | solution.py:79
  257.4 18.3 %copy.89 = bf16[512,1,4096]{0,2,1:T(8,128)(2,1)} copy(bf16[512,1,4096]{2,1,0:T(2,128)(2,1)} %get-tuple-element.20) | data formatting | bytes 8388608 | tf_op jit(solution)/shard_map/slice | solution.py:79
  275.8 4.8 copy.90
  280.6 18.3 %copy.86 = bf16[512,1,4096]{0,2,1:T(8,128)(2,1)} copy(bf16[512,1,4096]{2,1,0:T(2,128)(2,1)} %get-tuple-element.21) | data formatting | bytes 8388608 | tf_op jit(solution)/shard_map/slice | solution.py:78
  298.9 4.7 copy.87
  303.6 27.8 %reshape.260 = bf16[4096,4,512]{2,1,0:T(4,128)(2,1)} reshape(bf16[4096,2048]{1,0:T(8,128)(2,1)} %all-gather.8.cloned.1.call-done) | data formatting | bytes 33554432 | tf_op jit(solution)/shard_map/reshape | solution.py:76
  331.4 8.1 %slice.174 = bf16[4096,4,256]{2,1,0:T(4,128)(2,1)} slice(bf16[4096,4,512]{2,1,0:T(4,128)(2,1)} %reshape.260), slice={[0:4096], [0:4], [0:256]} | slice | bytes 16777216 | tf_op jit(solution)/shard_map/slice | solution.py:76
  339.5 9.3 %copy.112 = bf16[512,8,4,256]{3,1,2,0:T(8,128)(2,1)} copy(bf16[512,8,4,256]{3,2,1,0:T(4,128)(2,1)} %bitcast.96) | data formatting | bytes 16777216
  348.9 8.6 %fusion.47 = f32[512,1024]{0,1:T(8,128)S(1)} fusion(bf16[512,4096]{0,1:T(8,128)(2,1)} %bitcast.106, bf16[4096,1024]{1,0:T(8,128)(2,1)} %bitcast.101), kind=kOutput, calls=%fused_computation.127 | convolution fusion | flops 4294967296 | bytes 14680064 | tf_op jit(solution)/shard_map/dot_general | solution.py:79
  357.5 4.5 fusion.46
  362.7 11.7 %cholesky.50 = f32[128,128]{1,0:T(8,128)S(1)} custom-call(f32[128,128]{1,0:T(8,128)S(1)} %cholesky.118), custom_call_target="Cholesky" | custom-call | tf_op jit(solution)/shard_map/jit(cholesky)/cholesky | solution.py:81
  375.1 9.8 %custom-call.14 = f32[1,128,128]{1,2,0:T(8,128)S(1)} custom-call(f32[1,128,128]{2,1,0:T(8,128)S(1)} %get-tuple-element.27), custom_call_target="InvertDiagBlocksLowerTriangular" | custom-call | tf_op jit(solution)/shard_map/jit(cholesky)/cholesky | solution.py:81
  385.4 11.9 %cholesky.105 = f32[128,128]{1,0:T(8,128)S(1)} custom-call(f32[128,128]{1,0:T(8,128)S(1)} %convolution_subtract_fusion.2), custom_call_target="Cholesky" | custom-call | tf_op jit(solution)/shard_map/jit(cholesky)/cholesky | solution.py:81
  399.4 4.0 while.1
  400.0 1.4 bitcast_dynamic-update-slice_fusion.2
  402.0 1.4 bitcast_dynamic-update-slice_fusion.2
  403.4 19.7 %custom-call.15 = f32[2,128,128]{1,2,0:T(8,128)S(1)} custom-call(f32[2,128,128]{2,1,0:T(8,128)S(1)} %get-tuple-element.9), custom_call_target="InvertDiagBlocksLowerTriangular" | custom-call | tf_op jit(solution)/shard_map/triangular_solve | solution.py:82
  424.6 13.1 %convolution_bitcast_fusion.1 = f32[512,2048]{0,1:T(8,128)S(1)} fusion(bf16[4096,2048]{1,0:T(8,128)(2,1)} %all-gather.8.cloned.1.call-done, bf16[512,4096]{0,1:T(8,128)(2,1)} %bitcast.105), kind=kOutput, calls=%fused_computation.11 | convolution fusion | flops 8589934592 | bytes 25165824 | tf_op jit(solution)/shard_map/dot_general | solution.py:72
  437.7 11.9 %convolution_bitcast_fusion = f32[512,2048]{0,1:T(8,128)S(1)} fusion(bf16[4096,2048]{1,0:T(8,128)(2,1)} %all-gather.8.cloned.1.call-done, bf16[512,4096]{0,1:T(8,128)(2,1)S(1)} %bitcast.104), kind=kOutput, calls=%fused_computation.10 | convolution fusion | flops 8589934592 | bytes 25165824 | tf_op jit(solution)/shard_map/dot_general | solution.py:73
  449.6 1.0 fusion.3
  452.3 2.6 stack.34
  455.0 2.6 stack.33
  457.6 8.6 %maximum_bitcast_fusion = f32[8,16,2,16,32,2]{3,1,5,0,4,2:T(8,128)} fusion(f32[32,8,2,1,16,16]{5,4,2,1,0,3:T(8,128)} %stack.34, f32[32,8,2,1,16,16]{5,4,2,1,0,3:T(8,128)} %stack.33), kind=kLoop, calls=%fused_computation.7 | loop fusion | flops 262144 | bytes 2097152 | tf_op jit(solution)/shard_map/transpose | solution.py:32
  466.1 9.4 %copy.103 = f32[8,16,2,16,32,2]{1,0,5,4,3,2:T(8,128)} copy(f32[8,16,2,16,32,2]{3,1,5,0,4,2:T(8,128)} %maximum_bitcast_fusion) | data formatting | bytes 2097152 | tf_op jit(solution)/shard_map/transpose | solution.py:32
  475.5 5.6 %all_to_all.8 = f32[128,1,2048]{0,2,1:T(8,128)S(1)} reshape(f32[8,16,2,16,32,2]{1,0,5,4,3,2:T(8,128)} %copy.103) | data formatting | bytes 2097152 | tf_op jit(solution)/shard_map/all_to_all | solution.py:33
  481.1 1.9 copy.104
  483.0 8.4 %all-to-all-start = ((f32[128,1,2048]{2,1,0:T(1,128)}), f32[128,1,2048]{2,1,0:T(1,128)S(1)}, u32[]{:S(2)}, u32[]{:S(2)}) async-start(f32[128,1,2048]{2,1,0:T(1,128)} %copy.104), calls=%async_computation | async-start | bytes 2097152 | tf_op jit(solution)/shard_map/all_to_all | solution.py:33
  491.5 19.5 %all-to-all-done = f32[128,1,2048]{2,1,0:T(1,128)S(1)} async-done(((f32[128,1,2048]{2,1,0:T(1,128)}), f32[128,1,2048]{2,1,0:T(1,128)S(1)}, u32[]{:S(2)}, u32[]{:S(2)}) %all-to-all-start) | async-done | bytes 1048608 | tf_op jit(solution)/shard_map/all_to_all | solution.py:33
  511.3 1.0 gather_fusion.3
  513.3 1.2 squeeze.8
  514.5 1.2 squeeze.7
  (63 shorter events, 11.5 us)
Async XLA Ops:
  7.2 93.9 %all-gather.4.cloned.1.call-start = ((), (), s32[]{:S(2)}) async-start(), calls=%async_computation.1 | async-start | bytes 8912896 | tf_op jit(solution)/shard_map/all_gather | solution.py:21
  41.6 117.2 %all-gather.6.cloned.1.call-start = ((), (), s32[]{:S(2)}) async-start(), calls=%async_computation.2 | async-start | bytes 1179648 | tf_op jit(solution)/shard_map/all_gather | solution.py:20
  113.3 190.3 %all-gather.8.cloned.1.call-start = ((), (), s32[]{:S(2)}) async-start(), calls=%async_computation.3 | async-start | bytes 17825792 | tf_op jit(solution)/shard_map/all_gather | solution.py:21
  172.0 4.9 copy-start.1
  172.0 7.3 %copy-start = (s32[128]{0:T(128)S(1)}, s32[128]{0:T(128)}, u32[]{:S(2)}) copy-start(s32[128]{0:T(128)} %param.10) | copy-start | bytes 1540
  348.9 8.6 %copy-start.2 = (bf16[512,8,4,256]{3,1,2,0:T(8,128)(2,1)S(1)}, bf16[512,8,4,256]{3,1,2,0:T(8,128)(2,1)}, u32[]{:S(2)}) copy-start(bf16[512,8,4,256]{3,1,2,0:T(8,128)(2,1)} %copy.112) | copy-start | bytes 25165828
  348.9 8.6 %copy-start.4 = (bf16[512,16,8,32]{0,3,2,1:T(8,128)(2,1)S(1)}, bf16[512,16,8,32]{0,3,2,1:T(8,128)(2,1)}, u32[]{:S(2)}) copy-start(bf16[512,16,8,32]{0,3,2,1:T(8,128)(2,1)} %copy.87) | copy-start | bytes 12582916
  424.6 13.1 %copy-start.3 = (bf16[512,16,8,32]{0,3,2,1:T(8,128)(2,1)S(1)}, bf16[512,16,8,32]{0,3,2,1:T(8,128)(2,1)}, u32[]{:S(2)}) copy-start(bf16[512,16,8,32]{0,3,2,1:T(8,128)(2,1)} %copy.84) | copy-start | bytes 12582916
  483.0 28.0 %all-to-all-start = ((f32[128,1,2048]{2,1,0:T(1,128)}), f32[128,1,2048]{2,1,0:T(1,128)S(1)}, u32[]{:S(2)}, u32[]{:S(2)}) async-start(f32[128,1,2048]{2,1,0:T(1,128)} %copy.104), calls=%async_computation | async-start | bytes 2097152 | tf_op jit(solution)/shard_map/all_to_all | solution.py:33
Sparse Core Ops, SparseCore 0:
  41.8 59.3 all-gather.3
  113.4 45.3 all-gather.5
  160.6 92.3 all-gather.7

commit v3 on v2

--- a/solution.py
+++ b/solution.py
@@ -49,7 +49,14 @@
     panel_left = lax.dynamic_slice_in_dim(left_vecs, first_slot, per_device, 0)
     panel_right = lax.dynamic_slice_in_dim(right_vecs, first_slot, per_device, 0)
     panel_pairs = jnp.stack([panel_left, panel_right], axis=1)
-    matrices = jnp.stack([primal, dual_inverse], axis=0)
+    moves = [
+        ((q * grid_rows + p), (p * grid_cols + q))
+        for p in range(grid_rows)
+        for q in range(grid_cols)
+    ]
+    matrices = lax.ppermute(
+        jnp.stack([primal, dual_inverse], axis=0), ("prow", "pcol"), perm=moves
+    )
     gathered_pairs = gather_all(panel_pairs)
     raw_images = jnp.einsum(
         "gfn,mcn->gfmc", matrices, gathered_pairs, preferred_element_type=jnp.float32
@@ -63,21 +70,14 @@
     feature_rows = ordered.shape[1]
     images = ordered.transpose(1, 0, 3, 2).reshape(feature_rows, 8 * PANEL).astype(jnp.bfloat16)
     piece = gather_all(images)
-
-    def feature_order(vecs):
-        rows = vecs.shape[0]
-        vecs = vecs.reshape(rows, grid_rows, grid_cols, feature_rows)
-        return vecs.transpose(0, 2, 1, 3).reshape(rows, grid_rows * grid_cols * feature_rows)
-
-    left_prod = jnp.dot(feature_order(left_vecs), piece, preferred_element_type=jnp.float32)
-    right_prod = jnp.dot(feature_order(right_vecs), piece, preferred_element_type=jnp.float32)
+    left_prod = jnp.dot(left_vecs, piece, preferred_element_type=jnp.float32)
+    right_prod = jnp.dot(right_vecs, piece, preferred_element_type=jnp.float32)
     schur = combine(left_prod, right_prod)
     panel_vecs = jnp.take(gathered_pairs, gathered_ids, axis=0)
-    half = piece.reshape(piece.shape[0], 4, 2 * PANEL)[:, :, :PANEL].reshape(piece.shape[0], 4 * PANEL)
     panel_block = combine(
-        jnp.dot(feature_order(panel_vecs[:, 0]), half, preferred_element_type=jnp.float32),
-        jnp.dot(feature_order(panel_vecs[:, 1]), half, preferred_element_type=jnp.float32),
-    )
+        jnp.dot(panel_vecs[:, 0], piece, preferred_element_type=jnp.float32),
+        jnp.dot(panel_vecs[:, 1], piece, preferred_element_type=jnp.float32),
+    )[:, :PANEL]
     chol = jnp.linalg.cholesky(panel_block[:PANEL])
     inverse = lax.linalg.triangular_solve(
         chol, jnp.eye(PANEL, dtype=jnp.float32), left_side=True, lower=True

time: 530 us -> 493 us (0.930)
  local copies, waits for them, and re-layouts: 219 us -> 107 us
  waiting for transfers between devices: 120 us -> 159 us
  matrix products: 47.5 us -> 71.2 us
  starting transfers between devices: 9.03 us -> 18.8 us
    reshape x1 -> x0, local copies, waits for them, and re-layouts: 27.8 us -> none  [body(): piece.reshape(piece.shape[0], 4, 2 * PANEL)[:, :, :PANEL]]
    slice x2 -> x0, local copies, waits for them, and re-layouts: 26.4 us -> none  [the longest x1 18.3 us: body(): panel_vecs[:, 0]]
    dot_general x4, matrix products: 38.1 us -> 62 us  [the longest x1 18.6 us: body(): jnp.dot(panel_vecs[:, 0], piece, preferred_element_type=jnp.float32)]
    unnamed x14 -> x5, local copies, waits for them, and re-layouts: 22.8 us -> 0.35 us
    all_gather x1, waiting for transfers between devices: 45 us -> 65.7 us  [gather_all(): x = lax.all_gather(x, 'prow', axis=0, tiled=True)]
    slice x2 -> x1, local copies, waits for them, and re-layouts: 38.2 us -> 19.9 us  [body(): panel_vecs[:, 1]]
    transpose x4 -> x0, local copies, waits for them, and re-layouts: 16.9 us -> none  [feature_order(): vecs.transpose(0, 2, 1, 3)]
    ppermute x0 -> x1, starting transfers between devices: none -> 9.57 us  [body(): lax.ppermute(jnp.stack([primal, dual_inverse], axis=0), ('prow', 'pcol'),...]
  transfers between devices with their start and end apart: 4 -> 5, of which waited for: 3 -> 5; matrix products, arithmetic and copies ran while one was open for 28% -> 17% of each run, Pallas kernels for 0% -> 0%
where the time goes in v3:
time: 493 us; the launch traced here: 488 us
  waiting for transfers between devices  159 us (32%)
  local copies, waits for them, and re-layouts  107 us (22%)
  other arithmetic  83.9 us (17%)
  matrix products  71.2 us (14%)
  blocking collectives  31.5 us (6%)
  starting transfers between devices  18.8 us (4%)
  between operations  16.3 us (3%)
    all_gather x1, waiting for transfers between devices, gather_all(): x = lax.all_gather(x, 'prow', axis=0, tiled=True)  65.7 us
    all_gather x2, waiting for transfers between devices, gather_all(): return lax.all_gather(x, 'pcol', axis=0, tiled=True)  65 us
    another operation x7, other arithmetic, body(): chol = jnp.linalg.cholesky(panel_block[:PANEL])  34.6 us
    all_gather x1, blocking collectives, gather_all(): x = lax.all_gather(x, 'prow', axis=0, tiled=True)  31.5 us
    gather x1, local copies, waits for them, and re-layouts, body(): panel_vecs = jnp.take(gathered_pairs, gathered_ids, axis=0)  29.8 us
    slice x1, local copies, waits for them, and re-layouts, body(): panel_vecs[:, 1]  19.9 us
    another operation x3, other arithmetic, body(): lax.linalg.triangular_solve(chol, jnp.eye(PANEL, dtype=jnp.float32), left...  19.9 us
    all_to_all x1, waiting for transfers between devices, relay_rows(): lax.all_to_all(outgoing, ('prow', 'pcol'), split_axis=0, concat_axis=0, t...  19.5 us
  transfers between devices with their start and end apart: 5, of which 5 were waited for; matrix products, arithmetic and copies ran while one was open for 17% of the time, Pallas kernels for 0%

profile of v3, /device:TPU:1, one launch (start us, length us, event | category | flops | bytes accessed | tf_op | source)
XLA Modules:
  0.0 488.2 jit_solution(6881444465982047093)
XLA Ops:
  7.9 1.0 dynamic-slice_bitcast_fusion
  9.0 31.5 %all_gather.12 = bf16[32,2,4096]{2,1,0:T(2,128)(2,1)S(1)} all-gather(bf16[4,2,4096]{2,1,0:T(2,128)(2,1)S(1)} %copy.80), channel_id=1, replica_groups=mesh['prow'=8,'pcol'=16] {'prow'}, dimensions={0}, use_global_device_ids=true | all-gather | bytes 589824 | tf_op jit(solution)/shard_map/all_gather | solution.py:20
  40.5 1.1 copy.81
  41.7 1.1 pad_maximum_fusion
  42.8 9.6 %collective-permute-start = (bf16[2,32,4096]{2,1,0:T(8,128)(2,1)S(1)}, bf16[2,32,4096]{2,1,0:T(8,128)(2,1)S(1)}, u32[]{:S(2)}, u32[]{:S(2)}) collective-permute-start(bf16[2,32,4096]{2,1,0:T(8,128)(2,1)S(1)} %pad_maximum_fusion), channel_id=1, source_target_pairs={{0,0},{8,1},{16,2},{24,3},{32,4},{40,5},{48,6},{56,7},{64,8},{72,9... | collective-permute-start | bytes 1572872 | tf_op jit(solution)/shard_map/ppermute | solution.py:57
  52.4 3.4 gather_fusion
  55.9 9.2 %collective-permute-done = bf16[2,32,4096]{2,1,0:T(8,128)(2,1)S(1)} collective-permute-done((bf16[2,32,4096]{2,1,0:T(8,128)(2,1)S(1)}, bf16[2,32,4096]{2,1,0:T(8,128)(2,1)S(1)}, u32[]{:S(2)}, u32[]{:S(2)}) %collective-permute-start) | collective-permute-done | bytes 524320 | tf_op jit(solution)/shard_map/ppermute | solution.py:57
  65.1 49.0 %all-gather.4.cloned.1.call-done = bf16[512,2,4096]{2,0,1:T(8,128)(2,1)} async-done(((bf16[32,2,4096]{2,0,1:T(8,128)(2,1)}), bf16[512,2,4096]{2,0,1:T(8,128)(2,1)}) %all-gather.4.cloned.1.call-update) | async-done | bytes 8388624 | tf_op jit(solution)/shard_map/all_gather | solution.py:21
  114.0 6.0 %fusion = bf16[2,32,512,2]{2,1,3,0:T(8,128)(2,1)S(1)} fusion(bf16[512,2,4096]{2,0,1:T(8,128)(2,1)} %all-gather.4.cloned.1.call-done, bf16[2,32,4096]{2,1,0:T(8,128)(2,1)S(1)} %collective-permute-done), kind=kOutput, calls=%fused_computation.8 | convolution fusion | flops 536870912 | bytes 9043968 | tf_op jit(solution)/shard_map/gfn,mcn->gfmc/dot_general | solution.py:61
  120.5 2.3 gather_fusion.1
  122.8 1.8 fusion.17
  124.6 0.7 copy.83
  125.3 0.7 convert_element_type.12
  126.3 65.7 %all-gather.6.cloned.1.call-done = bf16[256,2048]{1,0:T(8,128)(2,1)} async-done(((bf16[32,2048]{1,0:T(8,128)(2,1)}), bf16[256,2048]{1,0:T(8,128)(2,1)}) %all-gather.6.cloned.1.call-update) | async-done | bytes 1048592 | tf_op jit(solution)/shard_map/all_gather | solution.py:20
  192.2 0.6 compare_select_fusion.7
  192.8 0.7 fusion.38
  193.5 16.4 %copy.84 = bf16[512,2,4096]{2,1,0:T(2,128)(2,1)} copy(bf16[512,2,4096]{2,0,1:T(8,128)(2,1)} %all-gather.4.cloned.1.call-done) | data formatting | bytes 16777216 | tf_op jit(solution)/shard_map/all_gather | solution.py:21
  209.9 29.8 %gather_fusion.2 = bf16[512,2,4096]{2,1,0:T(2,128)(2,1)} fusion(bf16[512,2,4096]{2,1,0:T(2,128)(2,1)} %copy.84, s32[1024]{0:T(1024)S(1)} %pad_clamp_fusion.1), kind=kCustom, calls=%fused_computation.2 | custom fusion | bytes 16779264 | tf_op jit(solution)/shard_map/jit(_take)/gather | solution.py:76
  239.7 10.5 %broadcast_select_fusion = bf16[512,2,4096]{2,1,0:T(2,128)(2,1)S(1)} fusion(bf16[512,2,4096]{2,1,0:T(2,128)(2,1)} %gather_fusion.2, pred[512]{0:T(512)(128)(4,1)S(1)} %compare_and_fusion), kind=kLoop, calls=%fused_computation.6 | loop fusion | flops 4194304 | bytes 16777728 | tf_op jit(solution)/shard_map/jit(_take)/select_n | solution.py:76
  250.3 19.9 %fusion.48 = (bf16[512,1,4096]{2,1,0:T(2,128)(2,1)}, bf16[512,1,4096]{2,1,0:T(2,128)(2,1)}) fusion(bf16[512,2,4096]{2,1,0:T(2,128)(2,1)S(1)} %broadcast_select_fusion), kind=kLoop, calls=%fused_computation.128 | loop fusion | bytes 16777216 | tf_op jit(solution)/shard_map/slice | solution.py:79
  270.2 16.0 %all-gather.8.cloned.1.call-done = bf16[4096,2048]{1,0:T(8,128)(2,1)} async-done(((bf16[256,2048]{1,0:T(8,128)(2,1)}), bf16[4096,2048]{1,0:T(8,128)(2,1)}) %all-gather.8.cloned.1.call-update) | async-done | bytes 16777232 | tf_op jit(solution)/shard_map/all_gather | solution.py:21
  286.2 18.2 %fusion.2 = f32[512,2048]{0,1:T(8,128)} fusion(bf16[4096,2048]{1,0:T(8,128)(2,1)} %all-gather.8.cloned.1.call-done, bf16[512,1,4096]{2,1,0:T(2,128)(2,1)} %get-tuple-element.20), kind=kOutput, calls=%fused_computation.10 | convolution fusion | flops 8589934592 | bytes 25165824 | tf_op jit(solution)/shard_map/dot_general | solution.py:79
  304.4 18.6 %fusion.5 = f32[512,2048]{0,1:T(8,128)} fusion(bf16[4096,2048]{1,0:T(8,128)(2,1)} %all-gather.8.cloned.1.call-done, bf16[512,1,4096]{2,1,0:T(2,128)(2,1)} %get-tuple-element.21), kind=kOutput, calls=%fused_computation.13 | convolution fusion | flops 8589934592 | bytes 25165824 | tf_op jit(solution)/shard_map/dot_general | solution.py:78
  322.9 4.4 fusion.9
  327.6 11.7 %cholesky.50 = f32[128,128]{1,0:T(8,128)S(1)} custom-call(f32[128,128]{1,0:T(8,128)S(1)} %cholesky.118), custom_call_target="Cholesky" | custom-call | tf_op jit(solution)/shard_map/jit(cholesky)/cholesky | solution.py:81
  339.4 9.8 %custom-call.14 = f32[1,128,128]{1,2,0:T(8,128)S(1)} custom-call(f32[1,128,128]{2,1,0:T(8,128)S(1)} %get-tuple-element.27), custom_call_target="InvertDiagBlocksLowerTriangular" | custom-call | tf_op jit(solution)/shard_map/jit(cholesky)/cholesky | solution.py:81
  349.7 11.7 %cholesky.105 = f32[128,128]{1,0:T(8,128)S(1)} custom-call(f32[128,128]{1,0:T(8,128)S(1)} %convolution_subtract_fusion.2), custom_call_target="Cholesky" | custom-call | tf_op jit(solution)/shard_map/jit(cholesky)/cholesky | solution.py:81
  361.4 0.6 compare_reduce_fusion
  364.1 4.0 while.1
  364.7 1.4 bitcast_dynamic-update-slice_fusion.2
  366.7 1.4 bitcast_dynamic-update-slice_fusion.2
  368.1 19.8 %custom-call.15 = f32[2,128,128]{1,2,0:T(8,128)S(1)} custom-call(f32[2,128,128]{2,1,0:T(8,128)S(1)} %get-tuple-element.9), custom_call_target="InvertDiagBlocksLowerTriangular" | custom-call | tf_op jit(solution)/shard_map/triangular_solve | solution.py:82
  389.4 13.2 %convolution_bitcast_fusion = f32[512,2048]{0,1:T(8,128)S(1)} fusion(bf16[4096,2048]{1,0:T(8,128)(2,1)} %all-gather.8.cloned.1.call-done, bf16[512,4096]{1,0:T(8,128)(2,1)} %param.7), kind=kOutput, calls=%fused_computation.16 | convolution fusion | flops 8589934592 | bytes 25165824 | tf_op jit(solution)/shard_map/dot_general | solution.py:74
  402.6 12.0 %convolution_bitcast_fusion.1 = f32[512,2048]{0,1:T(8,128)S(1)} fusion(bf16[4096,2048]{1,0:T(8,128)(2,1)} %all-gather.8.cloned.1.call-done, bf16[512,4096]{1,0:T(8,128)(2,1)S(1)} %copy-done.1), kind=kOutput, calls=%fused_computation.17 | convolution fusion | flops 8589934592 | bytes 25165824 | tf_op jit(solution)/shard_map/dot_general | solution.py:73
  414.7 1.0 fusion.12
  415.7 0.6 convolution_select_fusion
  416.6 0.6 fusion.8
  417.4 2.7 stack.34
  420.1 2.8 stack.33
  422.9 8.6 %maximum_bitcast_fusion = f32[8,16,2,16,32,2]{3,1,5,0,4,2:T(8,128)} fusion(f32[32,8,2,1,16,16]{5,4,2,1,0,3:T(8,128)} %stack.34, f32[32,8,2,1,16,16]{5,4,2,1,0,3:T(8,128)} %stack.33), kind=kLoop, calls=%fused_computation.7 | loop fusion | flops 262144 | bytes 2097152 | tf_op jit(solution)/shard_map/transpose | solution.py:32
  431.5 9.3 %copy.98 = f32[8,16,2,16,32,2]{1,0,5,4,3,2:T(8,128)} copy(f32[8,16,2,16,32,2]{3,1,5,0,4,2:T(8,128)} %maximum_bitcast_fusion) | data formatting | bytes 2097152 | tf_op jit(solution)/shard_map/transpose | solution.py:32
  440.8 5.6 %all_to_all.8 = f32[128,1,2048]{0,2,1:T(8,128)S(1)} reshape(f32[8,16,2,16,32,2]{1,0,5,4,3,2:T(8,128)} %copy.98) | data formatting | bytes 2097152 | tf_op jit(solution)/shard_map/all_to_all | solution.py:33
  446.4 1.9 copy.99
  448.3 8.8 %all-to-all-start = ((f32[128,1,2048]{2,1,0:T(1,128)}), f32[128,1,2048]{2,1,0:T(1,128)S(1)}, u32[]{:S(2)}, u32[]{:S(2)}) async-start(f32[128,1,2048]{2,1,0:T(1,128)} %copy.99), calls=%async_computation | async-start | bytes 2097152 | tf_op jit(solution)/shard_map/all_to_all | solution.py:33
  457.2 19.5 %all-to-all-done = f32[128,1,2048]{2,1,0:T(1,128)S(1)} async-done(((f32[128,1,2048]{2,1,0:T(1,128)}), f32[128,1,2048]{2,1,0:T(1,128)S(1)}, u32[]{:S(2)}, u32[]{:S(2)}) %all-to-all-start) | async-done | bytes 1048608 | tf_op jit(solution)/shard_map/all_to_all | solution.py:33
  477.0 1.0 gather_fusion.3
  479.0 1.2 squeeze.15
  480.2 1.2 squeeze.16
  (49 shorter events, 6.8 us)
Async XLA Ops:
  7.2 106.9 %all-gather.4.cloned.1.call-start = ((), (), s32[]{:S(2)}) async-start(), calls=%async_computation.1 | async-start | bytes 8912896 | tf_op jit(solution)/shard_map/all_gather | solution.py:21
  41.6 150.5 %all-gather.6.cloned.1.call-start = ((), (), s32[]{:S(2)}) async-start(), calls=%async_computation.2 | async-start | bytes 1179648 | tf_op jit(solution)/shard_map/all_gather | solution.py:20
  42.8 22.3 %collective-permute-start = (bf16[2,32,4096]{2,1,0:T(8,128)(2,1)S(1)}, bf16[2,32,4096]{2,1,0:T(8,128)(2,1)S(1)}, u32[]{:S(2)}, u32[]{:S(2)}) collective-permute-start(bf16[2,32,4096]{2,1,0:T(8,128)(2,1)S(1)} %pad_maximum_fusion), channel_id=1, source_target_pairs={{0,0},{8,1},{16,2},{24,3},{32,4},{40,5},{48,6},{56,7},{64,8},{72,9... | collective-permute-start | bytes 1572872 | tf_op jit(solution)/shard_map/ppermute | solution.py:57
  120.5 71.7 %copy-start = (s32[128]{0:T(128)S(1)}, s32[128]{0:T(128)}, u32[]{:S(2)}) copy-start(s32[128]{0:T(128)} %param.10) | copy-start | bytes 1540
  126.1 160.1 %all-gather.8.cloned.1.call-start = ((), (), s32[]{:S(2)}) async-start(), calls=%async_computation.3 | async-start | bytes 17825792 | tf_op jit(solution)/shard_map/all_gather | solution.py:21
  389.4 13.2 %copy-start.1 = (bf16[512,4096]{1,0:T(8,128)(2,1)S(1)}, bf16[512,4096]{1,0:T(8,128)(2,1)}, u32[]{:S(2)}) copy-start(bf16[512,4096]{1,0:T(8,128)(2,1)} %param.6) | copy-start | bytes 12582916
  448.3 28.4 %all-to-all-start = ((f32[128,1,2048]{2,1,0:T(1,128)}), f32[128,1,2048]{2,1,0:T(1,128)S(1)}, u32[]{:S(2)}, u32[]{:S(2)}) async-start(f32[128,1,2048]{2,1,0:T(1,128)} %copy.99), calls=%async_computation | async-start | bytes 2097152 | tf_op jit(solution)/shard_map/all_to_all | solution.py:33
Sparse Core Ops, SparseCore 0:
  41.8 72.2 all-gather.3
  126.2 65.8 all-gather.5
  193.8 92.3 all-gather.7

commit v4 on v3

--- a/solution.py
+++ b/solution.py
@@ -16,9 +16,20 @@
     )
 
 
+def gather_prow(x):
+    size = lax.axis_size("prow")
+    me = lax.axis_index("prow")
+    step = 1
+    while step < size:
+        got = lax.ppermute(x, "prow", perm=[(i, i ^ step) for i in range(size)])
+        low = (me & step) == 0
+        x = jnp.where(low, jnp.concatenate([x, got], axis=0), jnp.concatenate([got, x], axis=0))
+        step *= 2
+    return x
+
+
 def gather_all(x):
-    x = lax.all_gather(x, "prow", axis=0, tiled=True)
-    return lax.all_gather(x, "pcol", axis=0, tiled=True)
+    return lax.all_gather(gather_prow(x), "pcol", axis=0, tiled=True)
 
 
 def relay_rows(first_part, second_part, owner_map, devices, grid_rows):
@@ -48,7 +59,7 @@
     residue = jnp.sum(jnp.where(owner_map == me, jnp.arange(devices, dtype=jnp.int32), 0))
     panel_left = lax.dynamic_slice_in_dim(left_vecs, first_slot, per_device, 0)
     panel_right = lax.dynamic_slice_in_dim(right_vecs, first_slot, per_device, 0)
-    panel_pairs = jnp.stack([panel_left, panel_right], axis=1)
+    panel_pairs = jnp.concatenate([panel_left, panel_right], axis=0)
     moves = [
         ((q * grid_rows + p), (p * grid_cols + q))
         for p in range(grid_rows)
@@ -59,25 +70,31 @@
     )
     gathered_pairs = gather_all(panel_pairs)
     raw_images = jnp.einsum(
-        "gfn,mcn->gfmc", matrices, gathered_pairs, preferred_element_type=jnp.float32
+        "gfn,mn->gfm", matrices, gathered_pairs, preferred_element_type=jnp.float32
     )
     column_ids = jnp.arange(2 * PANEL, dtype=jnp.int32)
     owners = jnp.take(owner_map, column_ids % devices)
     gathered_ids = (
         (owners % grid_cols) * grid_rows + owners // grid_cols
-    ) * per_device + column_ids // devices
-    ordered = jnp.take(raw_images, gathered_ids, axis=2)
+    ) * (2 * per_device) + column_ids // devices
+    pair_ids = jnp.concatenate([gathered_ids, gathered_ids + per_device])
+    ordered = jnp.take(raw_images, pair_ids, axis=2)
     feature_rows = ordered.shape[1]
-    images = ordered.transpose(1, 0, 3, 2).reshape(feature_rows, 8 * PANEL).astype(jnp.bfloat16)
+    images = ordered.reshape(2 * feature_rows, 4 * PANEL)
+    images = images.reshape(2, feature_rows, 4 * PANEL).transpose(1, 0, 2)
+    images = images.reshape(feature_rows, 8 * PANEL).astype(jnp.bfloat16)
     piece = gather_all(images)
     left_prod = jnp.dot(left_vecs, piece, preferred_element_type=jnp.float32)
     right_prod = jnp.dot(right_vecs, piece, preferred_element_type=jnp.float32)
     schur = combine(left_prod, right_prod)
-    panel_vecs = jnp.take(gathered_pairs, gathered_ids, axis=0)
+    panel_prod = jnp.dot(gathered_pairs, piece, preferred_element_type=jnp.float32)
+    panel_prod = panel_prod.reshape(devices, 2, per_device, 8 * PANEL)
     panel_block = combine(
-        jnp.dot(panel_vecs[:, 0], piece, preferred_element_type=jnp.float32),
-        jnp.dot(panel_vecs[:, 1], piece, preferred_element_type=jnp.float32),
+        panel_prod[:, 0].reshape(devices * per_device, 8 * PANEL),
+        panel_prod[:, 1].reshape(devices * per_device, 8 * PANEL),
     )[:, :PANEL]
+    order_ids = (gathered_ids // (2 * per_device)) * per_device + gathered_ids % (2 * per_device)
+    panel_block = jnp.take(panel_block, order_ids, axis=0)
     chol = jnp.linalg.cholesky(panel_block[:PANEL])
     inverse = lax.linalg.triangular_solve(
         chol, jnp.eye(PANEL, dtype=jnp.float32), left_side=True, lower=True

time: 493 us -> 490 us (level)
  waiting for transfers between devices: 159 us -> 205 us
  blocking collectives: 31.5 us -> 0 us
  starting transfers between devices: 18.8 us -> 50.1 us
  local copies, waits for them, and re-layouts: 107 us -> 79.6 us
  matrix products: 71.2 us -> 58.5 us
  other arithmetic: 83.9 us -> 74.3 us
    ppermute x0 -> x6, starting transfers between devices: none -> 34.3 us  [gather_prow(): got = lax.ppermute(x, 'prow', perm=[(i, i ^ step) for i in range(size)])]
    all_gather x1 -> x0, blocking collectives: 31.5 us -> none  [gather_all(): x = lax.all_gather(x, 'prow', axis=0, tiled=True)]
    ppermute x0 -> x6, waiting for transfers between devices: none -> 27.7 us  [gather_prow(): got = lax.ppermute(x, 'prow', perm=[(i, i ^ step) for i in range(size)])]
    gather x2 -> x3, local copies, waits for them, and re-layouts: 32.1 us -> 5.68 us  [the longest x1 3.69 us: body(): ordered = jnp.take(raw_images, pair_ids, axis=2)]
    all_gather x2 -> x0, local copies, waits for them, and re-layouts: 17.5 us -> none  [the longest x1 16.4 us: gather_all(): return lax.all_gather(x, 'pcol', axis=0, tiled=True)]
    all_gather x3 -> x2, waiting for transfers between devices: 131 us -> 146 us  [gather_all(): return lax.all_gather(gather_prow(x), 'pcol', axis=0, tiled=True)]
    dot_general x3 -> x2, matrix products: 42.8 us -> 30.1 us  [the longest x1 24.1 us: body(): jnp.dot(gathered_pairs, piece, preferred_element_type=jnp.float32)]
    reshape x0 -> x1, local copies, waits for them, and re-layouts: none -> 9.82 us  [body(): panel_prod = panel_prod.reshape(devices, 2, per_device, 8 * PANEL)]
  transfers between devices with their start and end apart: 5 -> 10, of which waited for: 5 -> 10; matrix products, arithmetic and copies ran while one was open for 17% -> 1% of each run, Pallas kernels for 0% -> 0%
where the time goes in v4:
time: 490 us; the launch traced here: 484 us
  waiting for transfers between devices  205 us (42%)
  local copies, waits for them, and re-layouts  79.6 us (16%)
  other arithmetic  74.3 us (15%)
  matrix products  58.5 us (12%)
  starting transfers between devices  50.1 us (10%)
  between operations  16.7 us (3%)
    all_gather x2, waiting for transfers between devices, gather_all(): return lax.all_gather(gather_prow(x), 'pcol', axis=0, tiled=True)  146 us
    another operation x7, other arithmetic, body(): chol = jnp.linalg.cholesky(panel_block[:PANEL])  34.6 us
    ppermute x6, starting transfers between devices, gather_prow(): got = lax.ppermute(x, 'prow', perm=[(i, i ^ step) for i in range(size)])  34.3 us
    ppermute x6, waiting for transfers between devices, gather_prow(): got = lax.ppermute(x, 'prow', perm=[(i, i ^ step) for i in range(size)])  27.7 us
    dot_general x1, matrix products, body(): jnp.dot(gathered_pairs, piece, preferred_element_type=jnp.float32)  24.1 us
    another operation x3, other arithmetic, body(): lax.linalg.triangular_solve(chol, jnp.eye(PANEL, dtype=jnp.float32), left...  20.1 us
    all_to_all x1, waiting for transfers between devices, relay_rows(): lax.all_to_all(outgoing, ('prow', 'pcol'), split_axis=0, concat_axis=0, t...  19.5 us
    dot_general x1, matrix products, body(): right_prod = jnp.dot(right_vecs, piece, preferred_element_type=jnp.float32)  13.2 us
  transfers between devices with their start and end apart: 10, of which 10 were waited for; matrix products, arithmetic and copies ran while one was open for 1% of the time, Pallas kernels for 0%

profile of v4, /device:TPU:1, one launch (start us, length us, event | category | flops | bytes accessed | tf_op | source)
XLA Modules:
  0.0 484.3 jit_solution(11375538469749952186)
XLA Ops:
  9.0 2.5 collective-permute-start.1
  11.5 1.7 collective-permute-done.1
  13.2 3.5 collective-permute-start.2
  16.7 2.4 collective-permute-done.2
  19.1 2.8 collective-permute-start.3
  22.0 4.0 collective-permute-done.3
  28.0 6.9 %collective-permute-start = (bf16[2,32,4096]{2,1,0:T(8,128)(2,1)S(1)}, bf16[2,32,4096]{2,1,0:T(8,128)(2,1)S(1)}, u32[]{:S(2)}, u32[]{:S(2)}) collective-permute-start(bf16[2,32,4096]{2,1,0:T(8,128)(2,1)S(1)} %pad_maximum_fusion), channel_id=1, source_target_pairs={{0,0},{8,1},{16,2},{24,3},{32,4},{40,5},{48,6},{56,7},{64,8},{72,9... | collective-permute-start | bytes 1572872 | tf_op jit(solution)/shard_map/ppermute | solution.py:68
  35.0 3.3 gather_fusion
  38.4 11.6 %collective-permute-done = bf16[2,32,4096]{2,1,0:T(8,128)(2,1)S(1)} collective-permute-done((bf16[2,32,4096]{2,1,0:T(8,128)(2,1)S(1)}, bf16[2,32,4096]{2,1,0:T(8,128)(2,1)S(1)}, u32[]{:S(2)}, u32[]{:S(2)}) %collective-permute-start) | collective-permute-done | bytes 524320 | tf_op jit(solution)/shard_map/ppermute | solution.py:68
  50.0 49.9 %all-gather.3.cloned.1.call-done = bf16[1024,4096]{1,0:T(8,128)(2,1)} async-done(((bf16[64,4096]{1,0:T(8,128)(2,1)}), bf16[1024,4096]{1,0:T(8,128)(2,1)}) %all-gather.3.cloned.1.call-update) | async-done | bytes 8388624 | tf_op jit(solution)/shard_map/all_gather | solution.py:32
  99.9 6.0 %fusion = bf16[2,32,1024]{2,1,0:T(8,128)(2,1)S(1)} fusion(bf16[2,32,4096]{2,1,0:T(8,128)(2,1)S(1)} %collective-permute-done, bf16[1024,4096]{1,0:T(8,128)(2,1)} %all-gather.3.cloned.1.call-done), kind=kOutput, calls=%fused_computation.7 | convolution fusion | flops 536870912 | bytes 9043968 | tf_op jit(solution)/shard_map/gfn,mn->gfm/dot_general | solution.py:72
  106.4 3.7 gather_fusion.1
  110.1 3.7 fusion.10
  114.3 3.1 collective-permute-start.4
  117.4 3.6 collective-permute-done.4
  121.0 19.4 %collective-permute-start.5 = (bf16[64,2048]{1,0:T(8,128)(2,1)S(1)}, bf16[64,2048]{1,0:T(8,128)(2,1)S(1)}, u32[]{:S(2)}, u32[]{:S(2)}) collective-permute-start(bf16[64,2048]{1,0:T(8,128)(2,1)S(1)} %maximum_select_fusion.4), channel_id=1, source_target_pairs={{0,32},{16,48},{32,0},{48,16},{64,96},{80,112},{96,64},{112,80},{1... | collective-permute-start | bytes 786440 | tf_op jit(solution)/shard_map/ppermute | solution.py:24
  140.4 5.5 %collective-permute-done.5 = bf16[64,2048]{1,0:T(8,128)(2,1)S(1)} collective-permute-done((bf16[64,2048]{1,0:T(8,128)(2,1)S(1)}, bf16[64,2048]{1,0:T(8,128)(2,1)S(1)}, u32[]{:S(2)}, u32[]{:S(2)}) %collective-permute-start.5) | collective-permute-done | bytes 262176 | tf_op jit(solution)/shard_map/ppermute | solution.py:24
  146.0 2.9 collective-permute-start.6
  149.0 10.6 %collective-permute-done.6 = bf16[128,2048]{1,0:T(8,128)(2,1)S(1)} collective-permute-done((bf16[128,2048]{1,0:T(8,128)(2,1)S(1)}, bf16[128,2048]{1,0:T(8,128)(2,1)S(1)}, u32[]{:S(2)}, u32[]{:S(2)}) %collective-permute-start.6) | collective-permute-done | bytes 524320 | tf_op jit(solution)/shard_map/ppermute | solution.py:24
  159.6 1.3 maximum_select_fusion
  162.3 96.4 %all-gather.5.cloned.1.call-done = bf16[4096,2048]{1,0:T(8,128)(2,1)} async-done(((bf16[256,2048]{1,0:T(8,128)(2,1)}), bf16[4096,2048]{1,0:T(8,128)(2,1)}) %all-gather.5.cloned.1.call-update) | async-done | bytes 16777232 | tf_op jit(solution)/shard_map/all_gather | solution.py:32
  258.7 24.1 %fusion.51 = f32[1024,2048]{1,0:T(8,128)} fusion(bf16[1024,4096]{1,0:T(8,128)(2,1)} %all-gather.3.cloned.1.call-done, bf16[4096,2048]{1,0:T(8,128)(2,1)} %all-gather.5.cloned.1.call-done), kind=kOutput, calls=%fused_computation.152 | convolution fusion | flops 17179869184 | bytes 33554432 | tf_op jit(solution)/shard_map/dot_general | solution.py:90
  282.8 9.8 %reshape.373 = f32[128,2,4,2048]{3,2,1,0:T(4,128)} reshape(f32[1024,2048]{1,0:T(8,128)} %fusion.51) | data formatting | bytes 16777216 | tf_op jit(solution)/shard_map/reshape | solution.py:91
  292.6 10.4 %fusion.47 = (f32[128,1,4,2048]{3,2,1,0:T(4,128)}, f32[128,1,4,2048]{3,2,1,0:T(4,128)}) fusion(f32[128,2,4,2048]{3,2,1,0:T(4,128)} %reshape.373), kind=kLoop, calls=%fused_computation.148 | loop fusion | bytes 16777216 | tf_op jit(solution)/shard_map/slice | solution.py:94
  303.0 5.3 %reshape_squeeze.6 = f32[512,2048]{1,0:T(8,128)} reshape(f32[128,1,4,2048]{3,2,1,0:T(4,128)} %get-tuple-element.23) | data formatting | bytes 8388608 | tf_op jit(solution)/shard_map/reshape;squeeze | solution.py:93
  308.4 4.0 fusion.48
  312.3 5.3 %reshape_squeeze.7 = f32[512,2048]{1,0:T(8,128)} reshape(f32[128,1,4,2048]{3,2,1,0:T(4,128)} %get-tuple-element.22) | data formatting | bytes 8388608 | tf_op jit(solution)/shard_map/reshape;squeeze | solution.py:94
  317.7 2.8 fusion.49
  321.0 1.8 gather_fusion.2
  323.3 11.7 %cholesky.50 = f32[128,128]{1,0:T(8,128)S(1)} custom-call(f32[128,128]{1,0:T(8,128)S(1)} %cholesky.118), custom_call_target="Cholesky" | custom-call | tf_op jit(solution)/shard_map/jit(cholesky)/cholesky | solution.py:98
  335.0 9.8 %custom-call.14 = f32[1,128,128]{1,2,0:T(8,128)S(1)} custom-call(f32[1,128,128]{2,1,0:T(8,128)S(1)} %get-tuple-element.37), custom_call_target="InvertDiagBlocksLowerTriangular" | custom-call | tf_op jit(solution)/shard_map/jit(cholesky)/cholesky | solution.py:98
  345.3 11.7 %cholesky.105 = f32[128,128]{1,0:T(8,128)S(1)} custom-call(f32[128,128]{1,0:T(8,128)S(1)} %convolution_subtract_fusion.2), custom_call_target="Cholesky" | custom-call | tf_op jit(solution)/shard_map/jit(cholesky)/cholesky | solution.py:98
  359.8 4.0 while.1
  360.4 1.4 bitcast_dynamic-update-slice_fusion.2
  362.4 1.4 bitcast_dynamic-update-slice_fusion.2
  363.8 20.1 %custom-call.15 = f32[2,128,128]{1,2,0:T(8,128)S(1)} custom-call(f32[2,128,128]{2,1,0:T(8,128)S(1)} %get-tuple-element.9), custom_call_target="InvertDiagBlocksLowerTriangular" | custom-call | tf_op jit(solution)/shard_map/triangular_solve | solution.py:99
  385.3 13.2 %convolution_bitcast_fusion = f32[512,2048]{0,1:T(8,128)S(1)} fusion(bf16[4096,2048]{1,0:T(8,128)(2,1)} %all-gather.5.cloned.1.call-done, bf16[512,4096]{1,0:T(8,128)(2,1)} %param.7), kind=kOutput, calls=%fused_computation.9 | convolution fusion | flops 8589934592 | bytes 25165824 | tf_op jit(solution)/shard_map/dot_general | solution.py:88
  398.5 12.0 %convolution_bitcast_fusion.1 = f32[512,2048]{0,1:T(8,128)S(1)} fusion(bf16[4096,2048]{1,0:T(8,128)(2,1)} %all-gather.5.cloned.1.call-done, bf16[512,4096]{1,0:T(8,128)(2,1)S(1)} %copy-done.3), kind=kOutput, calls=%fused_computation.10 | convolution fusion | flops 8589934592 | bytes 25165824 | tf_op jit(solution)/shard_map/dot_general | solution.py:87
  413.3 2.6 stack.22
  416.0 2.8 stack.21
  418.7 8.6 %maximum_bitcast_fusion = f32[8,16,2,16,32,2]{3,1,5,0,4,2:T(8,128)} fusion(f32[32,8,2,1,16,16]{5,4,2,1,0,3:T(8,128)} %stack.22, f32[32,8,2,1,16,16]{5,4,2,1,0,3:T(8,128)} %stack.21), kind=kLoop, calls=%fused_computation.6 | loop fusion | flops 262144 | bytes 2097152 | tf_op jit(solution)/shard_map/transpose | solution.py:43
  427.3 9.4 %copy.34 = f32[8,16,2,16,32,2]{1,0,5,4,3,2:T(8,128)} copy(f32[8,16,2,16,32,2]{3,1,5,0,4,2:T(8,128)} %maximum_bitcast_fusion) | data formatting | bytes 2097152 | tf_op jit(solution)/shard_map/transpose | solution.py:43
  436.7 5.6 %all_to_all.8 = f32[128,1,2048]{0,2,1:T(8,128)S(1)} reshape(f32[8,16,2,16,32,2]{1,0,5,4,3,2:T(8,128)} %copy.34) | data formatting | bytes 2097152 | tf_op jit(solution)/shard_map/all_to_all | solution.py:44
  442.2 1.9 copy.35
  444.2 8.8 %all-to-all-start = ((f32[128,1,2048]{2,1,0:T(1,128)}), f32[128,1,2048]{2,1,0:T(1,128)S(1)}, u32[]{:S(2)}, u32[]{:S(2)}) async-start(f32[128,1,2048]{2,1,0:T(1,128)} %copy.35), calls=%async_computation | async-start | bytes 2097152 | tf_op jit(solution)/shard_map/all_to_all | solution.py:44
  453.1 19.5 %all-to-all-done = f32[128,1,2048]{2,1,0:T(1,128)S(1)} async-done(((f32[128,1,2048]{2,1,0:T(1,128)}), f32[128,1,2048]{2,1,0:T(1,128)S(1)}, u32[]{:S(2)}, u32[]{:S(2)}) %all-to-all-start) | async-done | bytes 1048608 | tf_op jit(solution)/shard_map/all_to_all | solution.py:44
  474.9 1.2 squeeze.7
  476.1 1.2 squeeze.8
  (73 shorter events, 16.2 us)
Async XLA Ops:
  7.2 27.8 %copy-start = (s32[128]{0:T(128)S(1)}, s32[128]{0:T(128)}, u32[]{:S(2)}) copy-start(s32[128]{0:T(128)} %param.10) | copy-start | bytes 1540
  7.2 92.8 %all-gather.3.cloned.1.call-start = ((), (), s32[]{:S(2)}) async-start(), calls=%async_computation.1 | async-start | bytes 8912896 | tf_op jit(solution)/shard_map/all_gather | solution.py:32
  9.0 4.2 collective-permute-start.1
  13.2 5.9 %collective-permute-start.2 = (bf16[16,4096]{1,0:T(8,128)(2,1)S(1)}, bf16[16,4096]{1,0:T(8,128)(2,1)S(1)}, u32[]{:S(2)}, u32[]{:S(2)}) collective-permute-start(bf16[16,4096]{1,0:T(8,128)(2,1)S(1)} %maximum_select_fusion.5), channel_id=1, source_target_pairs={{0,32},{16,48},{32,0},{48,16},{64,96},{80,112},{96,64},{112,80},{1... | collective-permute-start | bytes 393224 | tf_op jit(solution)/shard_map/ppermute | solution.py:24
  19.1 6.8 %collective-permute-start.3 = (bf16[32,4096]{1,0:T(8,128)(2,1)S(1)}, bf16[32,4096]{1,0:T(8,128)(2,1)S(1)}, u32[]{:S(2)}, u32[]{:S(2)}) collective-permute-start(bf16[32,4096]{1,0:T(8,128)(2,1)S(1)} %maximum_select_fusion.3), channel_id=1, source_target_pairs={{0,64},{16,80},{32,96},{48,112},{64,0},{80,16},{96,32},{112,48},{1... | collective-permute-start | bytes 786440 | tf_op jit(solution)/shard_map/ppermute | solution.py:24
  26.9 231.9 %all-gather.5.cloned.1.call-start = ((), (), s32[]{:S(2)}) async-start(), calls=%async_computation.2 | async-start | bytes 17825792 | tf_op jit(solution)/shard_map/all_gather | solution.py:32
  28.0 22.0 %collective-permute-start = (bf16[2,32,4096]{2,1,0:T(8,128)(2,1)S(1)}, bf16[2,32,4096]{2,1,0:T(8,128)(2,1)S(1)}, u32[]{:S(2)}, u32[]{:S(2)}) collective-permute-start(bf16[2,32,4096]{2,1,0:T(8,128)(2,1)S(1)} %pad_maximum_fusion), channel_id=1, source_target_pairs={{0,0},{8,1},{16,2},{24,3},{32,4},{40,5},{48,6},{56,7},{64,8},{72,9... | collective-permute-start | bytes 1572872 | tf_op jit(solution)/shard_map/ppermute | solution.py:68
  114.3 6.7 %collective-permute-start.4 = (bf16[32,2048]{1,0:T(8,128)(2,1)S(1)}, bf16[32,2048]{1,0:T(8,128)(2,1)S(1)}, u32[]{:S(2)}, u32[]{:S(2)}) collective-permute-start(bf16[32,2048]{1,0:T(8,128)(2,1)S(1)} %bitcast.74), channel_id=1, source_target_pairs={{0,16},{16,0},{32,48},{48,32},{64,80},{80,64},{96,112},{112,96},{1... | collective-permute-start | bytes 393224 | tf_op jit(solution)/shard_map/ppermute | solution.py:24
  121.0 24.9 %collective-permute-start.5 = (bf16[64,2048]{1,0:T(8,128)(2,1)S(1)}, bf16[64,2048]{1,0:T(8,128)(2,1)S(1)}, u32[]{:S(2)}, u32[]{:S(2)}) collective-permute-start(bf16[64,2048]{1,0:T(8,128)(2,1)S(1)} %maximum_select_fusion.4), channel_id=1, source_target_pairs={{0,32},{16,48},{32,0},{48,16},{64,96},{80,112},{96,64},{112,80},{1... | collective-permute-start | bytes 786440 | tf_op jit(solution)/shard_map/ppermute | solution.py:24
  146.0 13.5 %collective-permute-start.6 = (bf16[128,2048]{1,0:T(8,128)(2,1)S(1)}, bf16[128,2048]{1,0:T(8,128)(2,1)S(1)}, u32[]{:S(2)}, u32[]{:S(2)}) collective-permute-start(bf16[128,2048]{1,0:T(8,128)(2,1)S(1)} %maximum_select_fusion.2), channel_id=1, source_target_pairs={{0,64},{16,80},{32,96},{48,112},{64,0},{80,16},{96,32},{112,48},{1... | collective-permute-start | bytes 1572872 | tf_op jit(solution)/shard_map/ppermute | solution.py:24
  317.6 2.8 copy-start.1
  317.7 2.8 copy-start.2
  385.3 13.2 %copy-start.3 = (bf16[512,4096]{1,0:T(8,128)(2,1)S(1)}, bf16[512,4096]{1,0:T(8,128)(2,1)}, u32[]{:S(2)}) copy-start(bf16[512,4096]{1,0:T(8,128)(2,1)} %param.6) | copy-start | bytes 12582916
  444.2 28.4 %all-to-all-start = ((f32[128,1,2048]{2,1,0:T(1,128)}), f32[128,1,2048]{2,1,0:T(1,128)S(1)}, u32[]{:S(2)}, u32[]{:S(2)}) async-start(f32[128,1,2048]{2,1,0:T(1,128)} %copy.35), calls=%async_computation | async-start | bytes 2097152 | tf_op jit(solution)/shard_map/all_to_all | solution.py:44
Sparse Core Ops, SparseCore 0:
  27.0 72.9 all-gather.2
  161.0 97.6 all-gather.4

commit v5 on v4

--- a/solution.py
+++ b/solution.py
@@ -16,14 +16,16 @@
     )
 
 
-def gather_prow(x):
+def gather_prow(x, axis=0):
     size = lax.axis_size("prow")
     me = lax.axis_index("prow")
     step = 1
     while step < size:
         got = lax.ppermute(x, "prow", perm=[(i, i ^ step) for i in range(size)])
         low = (me & step) == 0
-        x = jnp.where(low, jnp.concatenate([x, got], axis=0), jnp.concatenate([got, x], axis=0))
+        x = jnp.where(
+            low, jnp.concatenate([x, got], axis=axis), jnp.concatenate([got, x], axis=axis)
+        )
         step *= 2
     return x
 
@@ -68,6 +70,7 @@
     matrices = lax.ppermute(
         jnp.stack([primal, dual_inverse], axis=0), ("prow", "pcol"), perm=moves
     )
+    matrices = gather_prow(matrices, axis=1)
     gathered_pairs = gather_all(panel_pairs)
     raw_images = jnp.einsum(
         "gfn,mn->gfm", matrices, gathered_pairs, preferred_element_type=jnp.float32
@@ -77,22 +80,30 @@
     gathered_ids = (
         (owners % grid_cols) * grid_rows + owners // grid_cols
     ) * (2 * per_device) + column_ids // devices
-    pair_ids = jnp.concatenate([gathered_ids, gathered_ids + per_device])
-    ordered = jnp.take(raw_images, pair_ids, axis=2)
-    feature_rows = ordered.shape[1]
-    images = ordered.reshape(2 * feature_rows, 4 * PANEL)
-    images = images.reshape(2, feature_rows, 4 * PANEL).transpose(1, 0, 2)
-    images = images.reshape(feature_rows, 8 * PANEL).astype(jnp.bfloat16)
-    piece = gather_all(images)
-    left_prod = jnp.dot(left_vecs, piece, preferred_element_type=jnp.float32)
-    right_prod = jnp.dot(right_vecs, piece, preferred_element_type=jnp.float32)
-    schur = combine(left_prod, right_prod)
+    feature_rows = raw_images.shape[1]
+
+    def image_half(h):
+        ids = gathered_ids[h * PANEL : (h + 1) * PANEL]
+        ordered = jnp.take(raw_images, jnp.concatenate([ids, ids + per_device]), axis=2)
+        ordered = ordered.transpose(1, 0, 2).reshape(feature_rows, 4 * PANEL)
+        return lax.all_gather(ordered.astype(jnp.bfloat16), "pcol", axis=0, tiled=True)
+
+    piece = image_half(0)
     panel_prod = jnp.dot(gathered_pairs, piece, preferred_element_type=jnp.float32)
-    panel_prod = panel_prod.reshape(devices, 2, per_device, 8 * PANEL)
+    panel_prod = panel_prod.reshape(devices, 2, per_device, 4 * PANEL)
     panel_block = combine(
-        panel_prod[:, 0].reshape(devices * per_device, 8 * PANEL),
-        panel_prod[:, 1].reshape(devices * per_device, 8 * PANEL),
-    )[:, :PANEL]
+        panel_prod[:, 0].reshape(devices * per_device, 4 * PANEL),
+        panel_prod[:, 1].reshape(devices * per_device, 4 * PANEL),
+    )
+    schur_first = combine(
+        jnp.dot(left_vecs, piece, preferred_element_type=jnp.float32),
+        jnp.dot(right_vecs, piece, preferred_element_type=jnp.float32),
+    )
+    piece = image_half(1)
+    schur_second = combine(
+        jnp.dot(left_vecs, piece, preferred_element_type=jnp.float32),
+        jnp.dot(right_vecs, piece, preferred_element_type=jnp.float32),
+    )
     order_ids = (gathered_ids // (2 * per_device)) * per_device + gathered_ids % (2 * per_device)
     panel_block = jnp.take(panel_block, order_ids, axis=0)
     chol = jnp.linalg.cholesky(panel_block[:PANEL])
@@ -105,16 +116,16 @@
         precision=lax.Precision.HIGHEST,
         preferred_element_type=jnp.float32,
     )
-    slots = schur.shape[0]
+    slots = schur_first.shape[0]
     schur_ids = jnp.arange(slots, dtype=jnp.int32) * devices + residue
     full = jnp.dot(
-        schur[:, :PANEL],
+        schur_first,
         inverse.T,
         precision=lax.Precision.HIGHEST,
         preferred_element_type=jnp.float32,
     )
     full = jnp.where((schur_ids >= start)[:, None], full, jnp.float32(0.0))
-    update = schur[:, PANEL:] - jnp.dot(
+    update = schur_second - jnp.dot(
         full, ahead.T, precision=lax.Precision.HIGHEST, preferred_element_type=jnp.float32
     )
     update = jnp.where((schur_ids >= start + PANEL)[:, None], update, jnp.float32(0.0))

time: 490 us -> 456 us (0.931)
  waiting for transfers between devices: 205 us -> 182 us
  local copies, waits for them, and re-layouts: 79.6 us -> 60.1 us
  starting transfers between devices: 50.1 us -> 59.9 us
    all_gather x2 -> x1, waiting for transfers between devices: 146 us -> 0.01 us  [gather_all(): return lax.all_gather(gather_prow(x), 'pcol', axis=0, tiled=True)]
    all_gather x0 -> x2, waiting for transfers between devices: none -> 63.7 us  [image_half(): lax.all_gather(ordered.astype(jnp.bfloat16), 'pcol', axis=0, tiled=True)]
    ppermute x6, waiting for transfers between devices: 27.7 us -> 83.8 us  [gather_prow(): got = lax.ppermute(x, 'prow', perm=[(i, i ^ step) for i in range(size)])]
    slice x3 -> x1, local copies, waits for them, and re-layouts: 17.2 us -> 5.21 us  [body(): panel_prod[:, 1].reshape(devices * per_device, 4 * PANEL)]
    ppermute x6, starting transfers between devices: 34.3 us -> 45 us  [gather_prow(): got = lax.ppermute(x, 'prow', perm=[(i, i ^ step) for i in range(size)])]
    dot_general x1, matrix products: 24.1 us -> 15.1 us  [body(): jnp.dot(gathered_pairs, piece, preferred_element_type=jnp.float32)]
    another operation x8, local copies, waits for them, and re-layouts: 14.6 us -> 9.02 us  [the longest x1 5.32 us: body(): panel_prod[:, 0].reshape(devices * per_device, 8 * PANEL)]
    dot_general x3 -> x5, matrix products: 25.8 us -> 29.6 us  [the longest x2 17 us: body(): jnp.dot(right_vecs, piece, preferred_element_type=jnp.float32)]
  transfers between devices with their start and end apart: 10 -> 11, of which waited for: 10 -> 9; matrix products, arithmetic and copies ran while one was open for 1% -> 28% of each run, Pallas kernels for 0% -> 0%
where the time goes in v5:
time: 456 us; the launch traced here: 449 us
  waiting for transfers between devices  182 us (40%)
  other arithmetic  73.6 us (16%)
  local copies, waits for them, and re-layouts  60.1 us (13%)
  starting transfers between devices  59.9 us (13%)
  matrix products  56.5 us (12%)
  between operations  16.6 us (4%)
    ppermute x6, waiting for transfers between devices, gather_prow(): got = lax.ppermute(x, 'prow', perm=[(i, i ^ step) for i in range(size)])  83.8 us
    all_gather x2, waiting for transfers between devices, image_half(): lax.all_gather(ordered.astype(jnp.bfloat16), 'pcol', axis=0, tiled=True)  63.7 us
    ppermute x6, starting transfers between devices, gather_prow(): got = lax.ppermute(x, 'prow', perm=[(i, i ^ step) for i in range(size)])  45 us
    another operation x7, other arithmetic, body(): chol = jnp.linalg.cholesky(panel_block[:PANEL])  34.6 us
    another operation x3, other arithmetic, body(): lax.linalg.triangular_solve(chol, jnp.eye(PANEL, dtype=jnp.float32), left...  19.9 us
    all_to_all x1, waiting for transfers between devices, relay_rows(): lax.all_to_all(outgoing, ('prow', 'pcol'), split_axis=0, concat_axis=0, t...  19.5 us
    dot_general x2, matrix products, body(): jnp.dot(right_vecs, piece, preferred_element_type=jnp.float32)  17 us
    ppermute x1, waiting for transfers between devices, body(): lax.ppermute(jnp.stack([primal, dual_inverse], axis=0), ('prow', 'pcol'),...  15.1 us
  transfers between devices with their start and end apart: 11, of which 9 were waited for; matrix products, arithmetic and copies ran while one was open for 28% of the time, Pallas kernels for 0%

profile of v5, /device:TPU:1, one launch (start us, length us, event | category | flops | bytes accessed | tf_op | source)
XLA Modules:
  0.0 448.9 jit_solution(16442357851373224201)
XLA Ops:
  9.0 2.5 collective-permute-start.4
  11.5 1.7 collective-permute-done.4
  13.2 3.5 collective-permute-start.5
  16.7 2.4 collective-permute-done.5
  19.1 2.8 collective-permute-start.6
  22.0 4.0 collective-permute-done.6
  28.0 6.9 %collective-permute-start = (bf16[2,32,4096]{2,1,0:T(8,128)(2,1)S(1)}, bf16[2,32,4096]{2,1,0:T(8,128)(2,1)S(1)}, u32[]{:S(2)}, u32[]{:S(2)}) collective-permute-start(bf16[2,32,4096]{2,1,0:T(8,128)(2,1)S(1)} %pad_maximum_fusion), channel_id=1, source_target_pairs={{0,0},{8,1},{16,2},{24,3},{32,4},{40,5},{48,6},{56,7},{64,8},{72,9... | collective-permute-start | bytes 1572872 | tf_op jit(solution)/shard_map/ppermute | solution.py:70
  34.9 15.1 %collective-permute-done = bf16[2,32,4096]{2,1,0:T(8,128)(2,1)S(1)} collective-permute-done((bf16[2,32,4096]{2,1,0:T(8,128)(2,1)S(1)}, bf16[2,32,4096]{2,1,0:T(8,128)(2,1)S(1)}, u32[]{:S(2)}, u32[]{:S(2)}) %collective-permute-start) | collective-permute-done | bytes 524320 | tf_op jit(solution)/shard_map/ppermute | solution.py:70
  50.0 17.9 %collective-permute-start.1 = (bf16[2,32,4096]{2,1,0:T(8,128)(2,1)S(1)}, bf16[2,32,4096]{2,1,0:T(8,128)(2,1)S(1)}, u32[]{:S(2)}, u32[]{:S(2)}) collective-permute-start(bf16[2,32,4096]{2,1,0:T(8,128)(2,1)S(1)} %collective-permute-done), channel_id=1, source_target_pairs={{0,16},{16,0},{32,48},{48,32},{64,80},{80,64},{96,112},{112,96},{1... | collective-permute-start | bytes 1572872 | tf_op jit(solution)/shard_map/ppermute | solution.py:24
  68.0 11.9 %collective-permute-done.1 = bf16[2,32,4096]{2,1,0:T(8,128)(2,1)S(1)} collective-permute-done((bf16[2,32,4096]{2,1,0:T(8,128)(2,1)S(1)}, bf16[2,32,4096]{2,1,0:T(8,128)(2,1)S(1)}, u32[]{:S(2)}, u32[]{:S(2)}) %collective-permute-start.1) | collective-permute-done | bytes 524320 | tf_op jit(solution)/shard_map/ppermute | solution.py:24
  80.1 15.5 %collective-permute-start.2 = (bf16[2,64,4096]{2,1,0:T(8,128)(2,1)S(1)}, bf16[2,64,4096]{2,1,0:T(8,128)(2,1)S(1)}, u32[]{:S(2)}, u32[]{:S(2)}) collective-permute-start(bf16[2,64,4096]{2,1,0:T(8,128)(2,1)S(1)} %maximum_select_fusion.3), channel_id=1, source_target_pairs={{0,32},{16,48},{32,0},{48,16},{64,96},{80,112},{96,64},{112,80},{1... | collective-permute-start | bytes 3145736 | tf_op jit(solution)/shard_map/ppermute | solution.py:24
  95.6 22.6 %collective-permute-done.2 = bf16[2,64,4096]{2,1,0:T(8,128)(2,1)S(1)} collective-permute-done((bf16[2,64,4096]{2,1,0:T(8,128)(2,1)S(1)}, bf16[2,64,4096]{2,1,0:T(8,128)(2,1)S(1)}, u32[]{:S(2)}, u32[]{:S(2)}) %collective-permute-start.2) | collective-permute-done | bytes 1048608 | tf_op jit(solution)/shard_map/ppermute | solution.py:24
  118.8 2.7 collective-permute-start.3
  121.5 3.3 gather_fusion
  124.9 41.3 %collective-permute-done.3 = bf16[2,128,4096]{2,1,0:T(8,128)(2,1)} collective-permute-done((bf16[2,128,4096]{2,1,0:T(8,128)(2,1)S(1)}, bf16[2,128,4096]{2,1,0:T(8,128)(2,1)}, u32[]{:S(2)}, u32[]{:S(2)}) %collective-permute-start.3) | collective-permute-done | bytes 2097184 | tf_op jit(solution)/shard_map/ppermute | solution.py:24
  166.2 9.2 %fusion = bf16[2,256,1024]{2,1,0:T(8,128)(2,1)S(1)} fusion(bf16[1024,4096]{1,0:T(8,128)(2,1)} %all-gather.4.cloned.1.call-done, bf16[2,128,4096]{2,1,0:T(8,128)(2,1)} %collective-permute-done.3, bf16[2,128,4096]{2,1,0:T(8,128)(2,1)S(1)} %maximum_select_fusion.2, pred[]{:T(512)S(6)} %eq.29), kind=kOutput, calls=%fused_computation.8 | convolution fusion | flops 4313841664 | bytes 13631489 | tf_op jit(solution)/shard_map/gfn,mn->gfm/dot_general | solution.py:75
  176.3 2.6 gather_fusion.3
  178.9 1.8 fusion.25
  182.1 2.6 gather_fusion.4
  184.7 1.8 fusion.26
  188.9 63.7 %all-gather.6.cloned.1.call-done = bf16[4096,1024]{0,1:T(8,128)(2,1)} async-done(((bf16[256,1024]{0,1:T(8,128)(2,1)}), bf16[4096,1024]{0,1:T(8,128)(2,1)}) %all-gather.6.cloned.1.call-update) | async-done | bytes 8388624 | tf_op jit(solution)/shard_map/all_gather | solution.py:89
  252.6 15.1 %fusion.67 = f32[1024,1024]{1,0:T(8,128)} fusion(bf16[1024,4096]{1,0:T(8,128)(2,1)} %all-gather.4.cloned.1.call-done, bf16[4096,1024]{0,1:T(8,128)(2,1)} %all-gather.6.cloned.1.call-done), kind=kOutput, calls=%fused_computation.176 | convolution fusion | flops 8589934592 | bytes 20971520 | tf_op jit(solution)/shard_map/dot_general | solution.py:92
  267.7 5.2 %reshape.311 = f32[128,2,4,1024]{3,2,1,0:T(4,128)} reshape(f32[1024,1024]{1,0:T(8,128)} %fusion.67) | data formatting | bytes 8388608 | tf_op jit(solution)/shard_map/reshape | solution.py:93
  272.9 5.2 %fusion.64 = (f32[128,1,4,1024]{3,2,1,0:T(4,128)}, f32[128,1,4,1024]{3,2,1,0:T(4,128)}) fusion(f32[128,2,4,1024]{3,2,1,0:T(4,128)} %reshape.311), kind=kLoop, calls=%fused_computation.173 | loop fusion | bytes 8388608 | tf_op jit(solution)/shard_map/slice | solution.py:96
  278.1 2.2 reshape_squeeze.6
  280.3 2.9 reshape_squeeze.7
  283.2 1.8 fusion.12
  285.0 1.7 gather_fusion.1
  287.3 11.7 %cholesky.50 = f32[128,128]{1,0:T(8,128)S(1)} custom-call(f32[128,128]{1,0:T(8,128)S(1)} %cholesky.118), custom_call_target="Cholesky" | custom-call | tf_op jit(solution)/shard_map/jit(cholesky)/cholesky | solution.py:109
  299.0 9.8 %custom-call.14 = f32[1,128,128]{1,2,0:T(8,128)S(1)} custom-call(f32[1,128,128]{2,1,0:T(8,128)S(1)} %get-tuple-element.30), custom_call_target="InvertDiagBlocksLowerTriangular" | custom-call | tf_op jit(solution)/shard_map/jit(cholesky)/cholesky | solution.py:109
  309.3 11.7 %cholesky.105 = f32[128,128]{1,0:T(8,128)S(1)} custom-call(f32[128,128]{1,0:T(8,128)S(1)} %convolution_subtract_fusion.2), custom_call_target="Cholesky" | custom-call | tf_op jit(solution)/shard_map/jit(cholesky)/cholesky | solution.py:109
  323.8 3.9 while.1
  324.4 1.4 bitcast_dynamic-update-slice_fusion.2
  326.4 1.4 bitcast_dynamic-update-slice_fusion.2
  327.7 19.9 %custom-call.15 = f32[2,128,128]{1,2,0:T(8,128)S(1)} custom-call(f32[2,128,128]{2,1,0:T(8,128)S(1)} %get-tuple-element.10), custom_call_target="InvertDiagBlocksLowerTriangular" | custom-call | tf_op jit(solution)/shard_map/triangular_solve | solution.py:110
  348.5 8.4 %convolution_bitcast_fusion.2 = f32[512,1024]{0,1:T(8,128)S(1)} fusion(bf16[4096,1024]{0,1:T(8,128)(2,1)} %all-gather.6.cloned.1.call-done, bf16[512,4096]{1,0:T(8,128)(2,1)} %param.9), kind=kOutput, calls=%fused_computation.20 | convolution fusion | flops 4294967296 | bytes 14680064 | tf_op jit(solution)/shard_map/dot_general | solution.py:100
  356.9 7.0 %convolution_bitcast_fusion.3 = f32[512,1024]{0,1:T(8,128)S(1)} fusion(bf16[4096,1024]{0,1:T(8,128)(2,1)} %all-gather.6.cloned.1.call-done, bf16[512,4096]{1,0:T(8,128)(2,1)S(1)} %copy-done.1), kind=kOutput, calls=%fused_computation.21 | convolution fusion | flops 4294967296 | bytes 14680064 | tf_op jit(solution)/shard_map/dot_general | solution.py:99
  365.0 2.6 stack.21
  368.3 8.6 %convolution_bitcast_fusion = f32[512,1024]{1,0:T(8,128)S(1)} fusion(bf16[4096,1024]{0,1:T(8,128)(2,1)} %all-gather.8.cloned.1.call-done, bf16[512,4096]{1,0:T(8,128)(2,1)} %param.9), kind=kOutput, calls=%fused_computation.18 | convolution fusion | flops 4294967296 | bytes 14680064 | tf_op jit(solution)/shard_map/dot_general | solution.py:105
  376.9 4.5 %convolution_bitcast_fusion.1 = f32[512,1024]{1,0:T(8,128)S(1)} fusion(bf16[4096,1024]{0,1:T(8,128)(2,1)S(1)} %copy-done.3, bf16[512,4096]{1,0:T(8,128)(2,1)S(1)} %copy-done.2), kind=kOutput, calls=%fused_computation.19 | convolution fusion | flops 4294967296 | bytes 14680064 | tf_op jit(solution)/shard_map/dot_general | solution.py:104
  382.2 2.6 stack.22
  384.8 8.6 %maximum_bitcast_fusion = f32[8,16,2,16,32,2]{3,1,5,0,4,2:T(8,128)} fusion(f32[32,8,2,1,16,16]{5,4,2,1,0,3:T(8,128)} %stack.22, f32[32,8,2,1,16,16]{5,4,2,1,0,3:T(8,128)} %stack.21), kind=kLoop, calls=%fused_computation.7 | loop fusion | flops 262144 | bytes 2097152 | tf_op jit(solution)/shard_map/transpose | solution.py:45
  393.4 9.4 %copy.34 = f32[8,16,2,16,32,2]{1,0,5,4,3,2:T(8,128)} copy(f32[8,16,2,16,32,2]{3,1,5,0,4,2:T(8,128)} %maximum_bitcast_fusion) | data formatting | bytes 2097152 | tf_op jit(solution)/shard_map/transpose | solution.py:45
  402.8 5.6 %all_to_all.8 = f32[128,1,2048]{0,2,1:T(8,128)S(1)} reshape(f32[8,16,2,16,32,2]{1,0,5,4,3,2:T(8,128)} %copy.34) | data formatting | bytes 2097152 | tf_op jit(solution)/shard_map/all_to_all | solution.py:46
  408.4 1.9 copy.35
  410.3 7.4 %all-to-all-start = ((f32[128,1,2048]{2,1,0:T(1,128)}), f32[128,1,2048]{2,1,0:T(1,128)S(1)}, u32[]{:S(2)}, u32[]{:S(2)}) async-start(f32[128,1,2048]{2,1,0:T(1,128)} %copy.35), calls=%async_computation | async-start | bytes 2097152 | tf_op jit(solution)/shard_map/all_to_all | solution.py:46
  417.7 19.5 %all-to-all-done = f32[128,1,2048]{2,1,0:T(1,128)S(1)} async-done(((f32[128,1,2048]{2,1,0:T(1,128)}), f32[128,1,2048]{2,1,0:T(1,128)S(1)}, u32[]{:S(2)}, u32[]{:S(2)}) %all-to-all-start) | async-done | bytes 1048608 | tf_op jit(solution)/shard_map/all_to_all | solution.py:46
  439.5 1.2 squeeze.7
  (75 shorter events, 19.2 us)
Async XLA Ops:
  7.2 159.0 %all-gather.4.cloned.1.call-start = ((), (), s32[]{:S(2)}) async-start(), calls=%async_computation.1 | async-start | bytes 8912896 | tf_op jit(solution)/shard_map/all_gather | solution.py:34
  9.0 4.2 collective-permute-start.4
  13.2 5.9 %collective-permute-start.5 = (bf16[16,4096]{1,0:T(8,128)(2,1)S(1)}, bf16[16,4096]{1,0:T(8,128)(2,1)S(1)}, u32[]{:S(2)}, u32[]{:S(2)}) collective-permute-start(bf16[16,4096]{1,0:T(8,128)(2,1)S(1)} %maximum_select_fusion.6), channel_id=1, source_target_pairs={{0,32},{16,48},{32,0},{48,16},{64,96},{80,112},{96,64},{112,80},{1... | collective-permute-start | bytes 393224 | tf_op jit(solution)/shard_map/ppermute | solution.py:24
  19.1 6.8 %collective-permute-start.6 = (bf16[32,4096]{1,0:T(8,128)(2,1)S(1)}, bf16[32,4096]{1,0:T(8,128)(2,1)S(1)}, u32[]{:S(2)}, u32[]{:S(2)}) collective-permute-start(bf16[32,4096]{1,0:T(8,128)(2,1)S(1)} %maximum_select_fusion.5), channel_id=1, source_target_pairs={{0,64},{16,80},{32,96},{48,112},{64,0},{80,16},{96,32},{112,48},{1... | collective-permute-start | bytes 786440 | tf_op jit(solution)/shard_map/ppermute | solution.py:24
  26.8 94.6 %copy-start = (s32[128]{0:T(128)S(1)}, s32[128]{0:T(128)}, u32[]{:S(2)}) copy-start(s32[128]{0:T(128)} %param.12) | copy-start | bytes 1540
  26.9 225.8 %all-gather.6.cloned.1.call-start = ((), (), s32[]{:S(2)}) async-start(), calls=%async_computation.2 | async-start | bytes 8912896 | tf_op jit(solution)/shard_map/all_gather | solution.py:89
  28.0 22.0 %collective-permute-start = (bf16[2,32,4096]{2,1,0:T(8,128)(2,1)S(1)}, bf16[2,32,4096]{2,1,0:T(8,128)(2,1)S(1)}, u32[]{:S(2)}, u32[]{:S(2)}) collective-permute-start(bf16[2,32,4096]{2,1,0:T(8,128)(2,1)S(1)} %pad_maximum_fusion), channel_id=1, source_target_pairs={{0,0},{8,1},{16,2},{24,3},{32,4},{40,5},{48,6},{56,7},{64,8},{72,9... | collective-permute-start | bytes 1572872 | tf_op jit(solution)/shard_map/ppermute | solution.py:70
  50.0 29.8 %collective-permute-start.1 = (bf16[2,32,4096]{2,1,0:T(8,128)(2,1)S(1)}, bf16[2,32,4096]{2,1,0:T(8,128)(2,1)S(1)}, u32[]{:S(2)}, u32[]{:S(2)}) collective-permute-start(bf16[2,32,4096]{2,1,0:T(8,128)(2,1)S(1)} %collective-permute-done), channel_id=1, source_target_pairs={{0,16},{16,0},{32,48},{48,32},{64,80},{80,64},{96,112},{112,96},{1... | collective-permute-start | bytes 1572872 | tf_op jit(solution)/shard_map/ppermute | solution.py:24
  80.1 38.2 %collective-permute-start.2 = (bf16[2,64,4096]{2,1,0:T(8,128)(2,1)S(1)}, bf16[2,64,4096]{2,1,0:T(8,128)(2,1)S(1)}, u32[]{:S(2)}, u32[]{:S(2)}) collective-permute-start(bf16[2,64,4096]{2,1,0:T(8,128)(2,1)S(1)} %maximum_select_fusion.3), channel_id=1, source_target_pairs={{0,32},{16,48},{32,0},{48,16},{64,96},{80,112},{96,64},{112,80},{1... | collective-permute-start | bytes 3145736 | tf_op jit(solution)/shard_map/ppermute | solution.py:24
  118.8 47.4 %collective-permute-start.3 = (bf16[2,128,4096]{2,1,0:T(8,128)(2,1)S(1)}, bf16[2,128,4096]{2,1,0:T(8,128)(2,1)}, u32[]{:S(2)}, u32[]{:S(2)}) collective-permute-start(bf16[2,128,4096]{2,1,0:T(8,128)(2,1)S(1)} %maximum_select_fusion.2), channel_id=1, source_target_pairs={{0,64},{16,80},{32,96},{48,112},{64,0},{80,16},{96,32},{112,48},{1... | collective-permute-start | bytes 6291464 | tf_op jit(solution)/shard_map/ppermute | solution.py:24
  181.6 186.7 %all-gather.8.cloned.1.call-start = ((), (), s32[]{:S(2)}) async-start(), calls=%async_computation.3 | async-start | bytes 8912896 | tf_op jit(solution)/shard_map/all_gather | solution.py:89
  348.5 8.4 %copy-start.1 = (bf16[512,4096]{1,0:T(8,128)(2,1)S(1)}, bf16[512,4096]{1,0:T(8,128)(2,1)}, u32[]{:S(2)}) copy-start(bf16[512,4096]{1,0:T(8,128)(2,1)} %param.8) | copy-start | bytes 12582916
  368.3 8.6 %copy-start.2 = (bf16[512,4096]{1,0:T(8,128)(2,1)S(1)}, bf16[512,4096]{1,0:T(8,128)(2,1)}, u32[]{:S(2)}) copy-start(bf16[512,4096]{1,0:T(8,128)(2,1)} %param.8) | copy-start | bytes 12582916
  368.3 8.6 %copy-start.3 = (bf16[4096,1024]{0,1:T(8,128)(2,1)S(1)}, bf16[4096,1024]{0,1:T(8,128)(2,1)}, u32[]{:S(2)}) copy-start(bf16[4096,1024]{0,1:T(8,128)(2,1)} %all-gather.8.cloned.1.call-done) | copy-start | bytes 25165828
  410.3 26.9 %all-to-all-start = ((f32[128,1,2048]{2,1,0:T(1,128)}), f32[128,1,2048]{2,1,0:T(1,128)S(1)}, u32[]{:S(2)}, u32[]{:S(2)}) async-start(f32[128,1,2048]{2,1,0:T(1,128)} %copy.35), calls=%async_computation | async-start | bytes 2097152 | tf_op jit(solution)/shard_map/all_to_all | solution.py:46
Sparse Core Ops, SparseCore 0:
  27.0 72.9 all-gather.3
  181.7 70.8 all-gather.5
  254.8 60.5 all-gather.7
